TPU v7x, 256 devices: a whole 4x4x8 slice. The times are simulated.
256 devices in a mesh: shot: 32 (over y, z_hi, core), depth: 8 (over x, z_lo).
Axes of the slice: x: 4, y: 4, z: 8 (z_hi: 4, z_lo: 2; z = z_hi * 2 + z_lo), core: 2. Of those that a mesh axis runs over, the one named last changes fastest.
Arguments:
- forward_start: bfloat16 [2, 32, 128, 128, 128], P(None, 'shot', 'depth'), may hold values from -6 to 6
- adjoint_end: bfloat16 [2, 32, 128, 128, 128], P(None, 'shot', 'depth'), may hold values from -6 to 6
- velocity: float32 [128, 128, 128], P('depth'), may hold values from 1.5 to 4.5
- source_cell: int32 [32], P('shot'), may hold values from 0 to 2097151
- wavelet: float32 [32, 4], P('shot'), may hold values from -16 to 16
- receiver_cell: int32 [32, 1024], P('shot'), may hold values from 0 to 2097151
- observed: float32 [32, 4, 1024], P('shot'), may hold values from -16 to 16
Outputs:
- forward_end: bfloat16 [2, 32, 128, 128, 128], P(None, 'shot', 'depth')
- adjoint_start: bfloat16 [2, 32, 128, 128, 128], P(None, 'shot', 'depth')
- velocity_new: float32 [128, 128, 128], P('depth')
All inputs are finite; a program needn't handle non-finite values.
Results may differ from a plain program's by a relative error of at most 0.0079.
Values may be sent and summed in bfloat16 or wider, within the bound.
No kernel may reach another device: no remote copies, remote signals or barrier semaphores. Data moves between devices by JAX's collectives and lax.ppermute only.
A program may use at most 64 MiB of HBM per device.

v0:
```python
import math

import jax
import jax.numpy as jnp
from jax import lax
from jax.sharding import PartitionSpec as P

CZ = 16
NX = 128
NY = 128
STEPS = 4


stencil_weights = (1.6, -0.2, 8.0 / 315.0, -1.0 / 560.0)
center_weight = -205.0 / 72.0
courant = 0.095
step_base = 0.01
low_speed = 1.5
high_speed = 4.5


def padded_2(cells, sides, width):
    for axis, dim in sides:
        count = lax.axis_size(axis)
        ends = count - 1
        head = lax.slice_in_dim(cells, 0, width, axis=dim)
        tail = lax.slice_in_dim(cells, cells.shape[dim] - width, cells.shape[dim], axis=dim)
        cells = jnp.concatenate(
            [
                lax.ppermute(tail, axis, [(i, (i + 1) % count) for i in range(ends)]),
                cells,
                lax.ppermute(head, axis, [((i + 1) % count, i) for i in range(ends)]),
            ],
            axis=dim,
        )
    return cells


def laplace(depth_padded):
    padded = jnp.pad(depth_padded, ((0, 0), (0, 0), (4, 4), (4, 4)))
    depth_len = padded.shape[1] - 8
    row_len = padded.shape[2] - 8
    column_len = padded.shape[3] - 8

    def window(along_z, along_x, along_y):
        return padded[
            :,
            4 + along_z : 4 + along_z + depth_len,
            4 + along_x : 4 + along_x + row_len,
            4 + along_y : 4 + along_y + column_len,
        ]

    summed = 3.0 * center_weight * window(0, 0, 0)
    for offset in range(1, 5):
        weight = stencil_weights[offset - 1]
        summed = summed + weight * (
            window(offset, 0, 0)
            + window(-offset, 0, 0)
            + window(0, offset, 0)
            + window(0, -offset, 0)
            + window(0, 0, offset)
            + window(0, 0, -offset)
        )
    return summed


def inject(wavefield, cell_ids, values, anchor):
    shot_count = wavefield.shape[0]
    depth_len = wavefield.shape[1]
    plane_size = NX * NY
    planes = cell_ids // plane_size - anchor
    owned_mask = (planes >= 0) & (planes < depth_len)
    flat_index = jnp.clip(planes, 0, depth_len - 1) * plane_size + cell_ids % plane_size
    rows_index = jnp.broadcast_to(jnp.arange(shot_count, dtype=jnp.int32)[:, None], cell_ids.shape)
    flattened = (
        wavefield.reshape(shot_count, -1)
        .at[rows_index, flat_index]
        .add(jnp.where(owned_mask, values, 0.0))
    )
    return flattened.reshape(wavefield.shape)


def record(wavefield, cell_ids, anchor):
    shot_count = wavefield.shape[0]
    plane_size = NX * NY
    planes = cell_ids // plane_size - anchor
    flat_index = jnp.clip(planes, 0, wavefield.shape[1] - 1) * plane_size + cell_ids % plane_size
    return jnp.take_along_axis(wavefield.reshape(shot_count, -1), flat_index, axis=1).astype(
        jnp.float32
    )


def body(forward_start, adjoint_end, velocity, source_cell, wavelet, receiver_cell, observed):
    anchor = lax.axis_index("depth") * CZ
    wave_model = (courant * velocity) ** 2
    source_ids = source_cell[:, None]
    images = []
    residuals = []
    earlier = forward_start[0]
    current = forward_start[1]
    for moment in range(STEPS):
        padded = padded_2(current, (("depth", 1),), 4)
        laplacian = laplace(padded.astype(jnp.float32))
        updated = (
            2.0 * current.astype(jnp.float32) - earlier.astype(jnp.float32) + wave_model * laplacian
        )
        updated = inject(updated, source_ids, wavelet[:, moment : moment + 1], anchor).astype(
            jnp.bfloat16
        )
        images.append(laplacian.astype(jnp.bfloat16))
        residuals.append(record(updated, receiver_cell, anchor) - observed[:, moment])
        earlier, current = (current, updated)
    images = list(lax.optimization_barrier(tuple(images)))
    nearer = adjoint_end[0]
    farther = adjoint_end[1]
    gradient = jnp.zeros(velocity.shape, jnp.float32)
    for moment in reversed(range(STEPS)):
        padded = padded_2(nearer, (("depth", 1),), 4)
        laplacian = laplace(padded.astype(jnp.float32))
        updated = (
            2.0 * nearer.astype(jnp.float32) - farther.astype(jnp.float32) + wave_model * laplacian
        )
        updated = inject(updated, receiver_cell, residuals[moment], anchor).astype(jnp.bfloat16)
        gradient = gradient + jnp.sum(
            updated.astype(jnp.float32) * images[moment].astype(jnp.float32), axis=0
        )
        farther, nearer = (nearer, updated)
    step_scale = step_base / math.sqrt(forward_start.shape[1] * lax.axis_size("shot"))
    summed = lax.psum(gradient, "shot")
    velocity_new = jnp.clip(velocity - step_scale * summed, low_speed, high_speed)
    forward_end = jnp.stack([earlier, current])
    adjoint_start = jnp.stack([nearer, farther])
    return (forward_end, adjoint_start, velocity_new)


def solution(mesh):
    placed = (
        P(None, "shot", "depth", None, None),
        P(None, "shot", "depth", None, None),
        P("depth", None, None),
        P("shot"),
        P("shot", None),
        P("shot", None),
        P("shot", None, None),
    )
    return jax.shard_map(
        body,
        mesh=mesh,
        in_specs=placed,
        out_specs=(
            P(None, "shot", "depth", None, None),
            P(None, "shot", "depth", None, None),
            P("depth", None, None),
        ),
        check_vma=False,
    )
```

profile of v0, /device:TPU:1, one launch (start us, length us, event | category | flops | bytes accessed | tf_op | source)
XLA Modules:
  0.0 539.2 jit_solution(1244440493901960534)
XLA Ops:
  7.3 1.2 slice_bitcast_fusion.1
  8.5 4.4 collective-permute-start
  12.8 1.3 collective-permute-start.1
  14.2 0.8 copy-done.20
  15.0 0.7 fusion.229
  15.7 4.0 collective-permute-start.8
  19.7 1.3 collective-permute-start.9
  21.2 0.7 fusion.234
  25.0 0.8 and_reduce_fusion.1
  26.1 3.0 fusion.223
  29.4 0.6 fusion.235
  32.0 10.9 %convert_reduce_fusion.3 = bf16[262144]{0:T(1024)(128)(2,1)S(1)} fusion(f32[1,262144]{1,0:T(1,128)S(1)} %scatter-add.48), kind=kLoop, calls=%fused_computation.413 | loop fusion | flops 262144 | bytes 1572864 | tf_op jit(solution)/shard_map/convert_element_type | solution.py:107
  42.9 4.2 collective-permute-start.2
  47.1 1.3 collective-permute-start.3
  48.4 0.6 collective-permute-done.2
  49.0 5.8 %collective-permute-done.3 = bf16[1,4,128,128]{3,2,1,0:T(8,128)(2,1)S(1)} collective-permute-done((bf16[1,4,128,128]{3,2,1,0:T(8,128)(2,1)S(1)}, bf16[1,4,128,128]{3,2,1,0:T(8,128)(2,1)S(1)}, u32[]{:S(2)}, u32[]{:S(2)}) %collective-permute-start.3) | collective-permute-done | bytes 131104 | tf_op jit(solution)/shard_map/ppermute | solution.py:32
  54.9 3.1 fusion.221
  58.3 0.6 fusion.236
  60.7 0.6 scatter-add.49
  61.3 10.9 %convert_reduce_fusion.2 = bf16[262144]{0:T(1024)(128)(2,1)S(1)} fusion(f32[1,262144]{1,0:T(1,128)S(1)} %scatter-add.49), kind=kLoop, calls=%fused_computation.412 | loop fusion | flops 262144 | bytes 1572864 | tf_op jit(solution)/shard_map/convert_element_type | solution.py:107
  72.2 3.2 collective-permute-start.4
  75.4 1.3 collective-permute-start.5
  76.7 11.4 %gather_fusion.3 = bf16[1024]{0:T(1024)(128)(2,1)} fusion(bf16[262144]{0:T(1024)(128)(2,1)S(1)} %convert_reduce_fusion.3, s32[1024]{0:T(1024)S(1)} %broadcast_clamp_fusion), kind=kCustom, calls=%fused_computation.3.clone | custom fusion | bytes 8192 | tf_op jit(solution)/shard_map/jit(take_along_axis)/gather | solution.py:88
  88.3 3.1 fusion.219
  91.6 0.7 fusion.237
  94.3 10.9 %convert_reduce_fusion.1 = bf16[262144]{0:T(1024)(128)(2,1)S(1)} fusion(f32[1,262144]{1,0:T(1,128)S(1)} %scatter-add.50), kind=kLoop, calls=%fused_computation.411 | loop fusion | flops 262144 | bytes 1572864 | tf_op jit(solution)/shard_map/convert_element_type | solution.py:107
  105.2 0.7 fusion.230
  105.9 4.0 collective-permute-start.6
  109.9 1.5 collective-permute-start.7
  111.4 1.2 maximum_convert_fusion.4
  112.6 13.5 %gather_fusion.2 = bf16[1024]{0:T(1024)(128)(2,1)S(1)} fusion(bf16[262144]{0:T(1024)(128)(2,1)} %copy-done.1, s32[1024]{0:T(1024)S(1)} %broadcast_clamp_fusion), kind=kCustom, calls=%fused_computation.2.clone | custom fusion | bytes 8192 | tf_op jit(solution)/shard_map/jit(take_along_axis)/gather | solution.py:88
  126.1 6.8 %gather_fusion.1 = bf16[1024]{0:T(1024)(128)(2,1)S(1)} fusion(bf16[262144]{0:T(1024)(128)(2,1)S(1)} %convert_reduce_fusion.1, s32[1024]{0:T(1024)S(1)} %broadcast_clamp_fusion), kind=kCustom, calls=%fused_computation.1.clone | custom fusion | bytes 8192 | tf_op jit(solution)/shard_map/jit(take_along_axis)/gather | solution.py:88
  132.9 1.0 maximum_convert_fusion.3
  133.9 3.1 fusion.217
  137.0 3.4 fusion.6
  140.4 1.0 copy-done.14
  141.4 0.6 fusion.238
  143.9 1.3 scatter-add.51
  145.1 12.0 %convert_reduce_fusion = bf16[262144]{0:T(1024)(128)(2,1)S(1)} fusion(f32[1,262144]{1,0:T(1,128)} %scatter-add.51), kind=kLoop, calls=%fused_computation.410 | loop fusion | flops 262144 | bytes 1572864 | tf_op jit(solution)/shard_map/convert_element_type | solution.py:107
  157.1 6.8 %gather_fusion = bf16[1024]{0:T(1024)(128)(2,1)S(1)} fusion(bf16[262144]{0:T(1024)(128)(2,1)S(1)} %convert_reduce_fusion, s32[1024]{0:T(1024)S(1)} %broadcast_clamp_fusion), kind=kCustom, calls=%fused_computation.clone | custom fusion | bytes 8192 | tf_op jit(solution)/shard_map/jit(take_along_axis)/gather | solution.py:88
  164.0 6.5 %scatter_fusion = f32[262144]{0:T(1024)S(1)} fusion(f32[262144]{0:T(1024)S(1)} %bitcast.100, s32[1024]{0:T(1024)S(1)} %broadcast_select_fusion, f32[1024]{0:T(1024)S(1)} %bitcast.136), kind=kCustom, calls=%fused_computation.4 | custom fusion | flops 1024 | bytes 16384
  170.6 5.0 collective-permute-start.10
  175.6 1.3 collective-permute-start.11
  176.9 0.6 collective-permute-done.10
  177.5 4.6 collective-permute-done.11
  182.3 2.4 fusion.7
  184.7 6.7 %scatter_fusion.1 = f32[262144]{0:T(1024)S(1)} fusion(f32[262144]{0:T(1024)S(1)} %bitcast.102, s32[1024]{0:T(1024)S(1)} %broadcast_select_fusion, f32[1024]{0:T(1024)S(1)} %bitcast.135), kind=kCustom, calls=%fused_computation.5 | custom fusion | flops 1024 | bytes 16384
  191.5 5.5 %collective-permute-start.12 = (bf16[1,4,128,128]{3,2,1,0:T(8,128)(2,1)S(1)}, bf16[1,4,128,128]{3,2,1,0:T(8,128)(2,1)S(1)}, u32[]{:S(2)}, u32[]{:S(2)}) collective-permute-start(bf16[1,4,128,128]{3,2,1,0:T(8,128)(2,1)S(1)} %get-tuple-element.74), channel_id=1, source_target_pairs={{0,1},{1,2},{2,3},{3,4},{4,5},{5,6},{6,7},{8,9},{9,10},{10,11},{11... | collective-permute-start | bytes 393224 | tf_op jit(solution)/shard_map/ppermute | solution.py:30
  197.0 1.3 collective-permute-start.13
  198.3 0.6 collective-permute-done.12
  198.9 4.8 collective-permute-done.13
  203.9 2.4 fusion.11
  206.3 6.5 %scatter_fusion.2 = f32[262144]{0:T(1024)S(1)} fusion(f32[262144]{0:T(1024)S(1)} %bitcast.103, s32[1024]{0:T(1024)S(1)} %broadcast_select_fusion, f32[1024]{0:T(1024)S(1)} %bitcast.134), kind=kCustom, calls=%fused_computation.6 | custom fusion | flops 1024 | bytes 16384
  212.9 1.9 collective-permute-start.14
  214.8 1.3 collective-permute-start.15
  216.1 0.6 collective-permute-done.14
  216.8 4.8 collective-permute-done.15
  221.7 2.4 fusion.13
  224.2 6.5 %scatter_fusion.3 = f32[262144]{0:T(1024)S(1)} fusion(f32[262144]{0:T(1024)S(1)} %bitcast.101, s32[1024]{0:T(1024)S(1)} %broadcast_select_fusion, f32[1024]{0:T(1024)S(1)} %bitcast.133), kind=kCustom, calls=%fused_computation.7 | custom fusion | flops 1024 | bytes 16384
  230.7 0.8 copy-done.13
  232.2 3.2 fusion.10
  235.4 2.5 pad_maximum_fusion
  237.9 291.8 %all-reduce.11.cloned.1.call-done = f32[16,128,128]{2,1,0:T(8,128)} async-done(((f32[16,128,128]{2,1,0:T(8,128)}), f32[16,128,128]{2,1,0:T(8,128)}) %all-reduce.11.cloned.1.call-update) | async-done | bytes 1048592 | tf_op jit(solution)/shard_map/psum | solution.py:129
  529.8 2.4 subtract_clamp_fusion
  (89 shorter events, 3.3 us)
Async XLA Ops:
  7.2 13.9 %copy-start.26 = (s32[2]{0:T(128)S(1)}, s32[2]{0:T(128)}, u32[]{:S(2)}) copy-start(s32[2]{0:T(128)} %constant.279) | copy-start | bytes 28
  7.2 18.6 %copy-start.25 = (s32[2]{0:T(128)S(1)}, s32[2]{0:T(128)}, u32[]{:S(2)}) copy-start(s32[2]{0:T(128)} %constant.276) | copy-start | bytes 28
  7.2 6.9 %copy-start.15 = (bf16[2,1,16,128,128]{4,3,2,1,0:T(8,128)(2,1)S(1)}, bf16[2,1,16,128,128]{4,3,2,1,0:T(8,128)(2,1)}, u32[]{:S(2)}) copy-start(bf16[2,1,16,128,128]{4,3,2,1,0:T(8,128)(2,1)} %param.18) | copy-start | bytes 3145732
  7.2 13.8 %copy-start.24 = (s32[1,1024]{1,0:T(1,128)S(1)}, s32[1,1024]{1,0:T(1,128)}, u32[]{:S(2)}) copy-start(s32[1,1024]{1,0:T(1,128)} %param.22) | copy-start | bytes 12292
  7.2 14.0 %copy-start.23 = (f32[1,4]{1,0:T(1,128)S(1)}, f32[1,4]{1,0:T(1,128)}, u32[]{:S(2)}) copy-start(f32[1,4]{1,0:T(1,128)} %param.21) | copy-start | bytes 52
  7.2 522.5 %all-reduce.11.cloned.1.call-start = ((), (), s32[]{:S(2)}) async-start(), calls=%async_computation | async-start | bytes 2097152 | tf_op jit(solution)/shard_map/psum | solution.py:129
  8.5 17.4 %collective-permute-start = (bf16[1,4,128,128]{3,2,1,0:T(8,128)(2,1)S(1)}, bf16[1,4,128,128]{3,2,1,0:T(8,128)(2,1)S(1)}, u32[]{:S(2)}, u32[]{:S(2)}) collective-permute-start(bf16[1,4,128,128]{3,2,1,0:T(8,128)(2,1)S(1)} %get-tuple-element.86), channel_id=1, source_target_pairs={{0,1},{1,2},{2,3},{3,4},{4,5},{5,6},{6,7},{8,9},{9,10},{10,11},{11... | collective-permute-start | bytes 393224 | tf_op jit(solution)/shard_map/ppermute | solution.py:30
  12.8 13.1 %collective-permute-start.1 = (bf16[1,4,128,128]{3,2,1,0:T(8,128)(2,1)S(1)}, bf16[1,4,128,128]{3,2,1,0:T(8,128)(2,1)S(1)}, u32[]{:S(2)}, u32[]{:S(2)}) collective-permute-start(bf16[1,4,128,128]{3,2,1,0:T(8,128)(2,1)S(1)} %get-tuple-element.87), channel_id=1, source_target_pairs={{1,0},{2,1},{3,2},{4,3},{5,4},{6,5},{7,6},{9,8},{10,9},{11,10},{12... | collective-permute-start | bytes 393224 | tf_op jit(solution)/shard_map/ppermute | solution.py:32
  14.2 0.8 copy-start.20
  15.7 95.7 %collective-permute-start.8 = (bf16[1,4,128,128]{3,2,1,0:T(8,128)(2,1)}, bf16[1,4,128,128]{3,2,1,0:T(8,128)(2,1)S(1)}, u32[]{:S(2)}, u32[]{:S(2)}) collective-permute-start(bf16[1,4,128,128]{3,2,1,0:T(8,128)(2,1)} %get-tuple-element.78), channel_id=1, source_target_pairs={{0,1},{1,2},{2,3},{3,4},{4,5},{5,6},{6,7},{8,9},{9,10},{10,11},{11... | collective-permute-start | bytes 393224 | tf_op jit(solution)/shard_map/ppermute | solution.py:30
  19.7 91.7 %collective-permute-start.9 = (bf16[1,4,128,128]{3,2,1,0:T(8,128)(2,1)}, bf16[1,4,128,128]{3,2,1,0:T(8,128)(2,1)S(1)}, u32[]{:S(2)}, u32[]{:S(2)}) collective-permute-start(bf16[1,4,128,128]{3,2,1,0:T(8,128)(2,1)} %get-tuple-element.79), channel_id=1, source_target_pairs={{1,0},{2,1},{3,2},{4,3},{5,4},{6,5},{7,6},{9,8},{10,9},{11,10},{12... | collective-permute-start | bytes 393224 | tf_op jit(solution)/shard_map/ppermute | solution.py:32
  26.0 3.1 copy-start
  26.1 3.1 copy-start.18
  42.9 6.1 %collective-permute-start.2 = (bf16[1,4,128,128]{3,2,1,0:T(8,128)(2,1)S(1)}, bf16[1,4,128,128]{3,2,1,0:T(8,128)(2,1)S(1)}, u32[]{:S(2)}, u32[]{:S(2)}) collective-permute-start(bf16[1,4,128,128]{3,2,1,0:T(8,128)(2,1)S(1)} %get-tuple-element.84), channel_id=1, source_target_pairs={{0,1},{1,2},{2,3},{3,4},{4,5},{5,6},{6,7},{8,9},{9,10},{10,11},{11... | collective-permute-start | bytes 393224 | tf_op jit(solution)/shard_map/ppermute | solution.py:30
  47.1 7.7 %collective-permute-start.3 = (bf16[1,4,128,128]{3,2,1,0:T(8,128)(2,1)S(1)}, bf16[1,4,128,128]{3,2,1,0:T(8,128)(2,1)S(1)}, u32[]{:S(2)}, u32[]{:S(2)}) collective-permute-start(bf16[1,4,128,128]{3,2,1,0:T(8,128)(2,1)S(1)} %get-tuple-element.85), channel_id=1, source_target_pairs={{1,0},{2,1},{3,2},{4,3},{5,4},{6,5},{7,6},{9,8},{10,9},{11,10},{12... | collective-permute-start | bytes 393224 | tf_op jit(solution)/shard_map/ppermute | solution.py:32
  54.9 3.1 copy-start.19
  72.2 19.2 %copy-start.1 = (bf16[262144]{0:T(1024)(128)(2,1)}, bf16[262144]{0:T(1024)(128)(2,1)S(1)}, u32[]{:S(2)}) copy-start(bf16[262144]{0:T(1024)(128)(2,1)S(1)} %convert_reduce_fusion.2) | copy-start | bytes 1572868
  72.2 15.9 %collective-permute-start.4 = (bf16[1,4,128,128]{3,2,1,0:T(8,128)(2,1)S(1)}, bf16[1,4,128,128]{3,2,1,0:T(8,128)(2,1)S(1)}, u32[]{:S(2)}, u32[]{:S(2)}) collective-permute-start(bf16[1,4,128,128]{3,2,1,0:T(8,128)(2,1)S(1)} %get-tuple-element.82), channel_id=1, source_target_pairs={{0,1},{1,2},{2,3},{3,4},{4,5},{5,6},{6,7},{8,9},{9,10},{10,11},{11... | collective-permute-start | bytes 393224 | tf_op jit(solution)/shard_map/ppermute | solution.py:30
  75.4 12.7 %collective-permute-start.5 = (bf16[1,4,128,128]{3,2,1,0:T(8,128)(2,1)S(1)}, bf16[1,4,128,128]{3,2,1,0:T(8,128)(2,1)S(1)}, u32[]{:S(2)}, u32[]{:S(2)}) collective-permute-start(bf16[1,4,128,128]{3,2,1,0:T(8,128)(2,1)S(1)} %get-tuple-element.83), channel_id=1, source_target_pairs={{1,0},{2,1},{3,2},{4,3},{5,4},{6,5},{7,6},{9,8},{10,9},{11,10},{12... | collective-permute-start | bytes 393224 | tf_op jit(solution)/shard_map/ppermute | solution.py:32
  105.9 27.0 %collective-permute-start.6 = (bf16[1,4,128,128]{3,2,1,0:T(8,128)(2,1)}, bf16[1,4,128,128]{3,2,1,0:T(8,128)(2,1)S(1)}, u32[]{:S(2)}, u32[]{:S(2)}) collective-permute-start(bf16[1,4,128,128]{3,2,1,0:T(8,128)(2,1)} %get-tuple-element.80), channel_id=1, source_target_pairs={{0,1},{1,2},{2,3},{3,4},{4,5},{5,6},{6,7},{8,9},{9,10},{10,11},{11... | collective-permute-start | bytes 393224 | tf_op jit(solution)/shard_map/ppermute | solution.py:30
  109.9 23.0 %collective-permute-start.7 = (bf16[1,4,128,128]{3,2,1,0:T(8,128)(2,1)}, bf16[1,4,128,128]{3,2,1,0:T(8,128)(2,1)}, u32[]{:S(2)}, u32[]{:S(2)}) collective-permute-start(bf16[1,4,128,128]{3,2,1,0:T(8,128)(2,1)} %get-tuple-element.81), channel_id=1, source_target_pairs={{1,0},{2,1},{3,2},{4,3},{5,4},{6,5},{7,6},{9,8},{10,9},{11,10},{12... | collective-permute-start | bytes 393224 | tf_op jit(solution)/shard_map/ppermute | solution.py:32
  133.9 3.1 copy-start.2
  133.9 3.1 copy-start.16
  140.4 1.0 copy-start.14
  145.1 18.8 %copy-start.21 = (f32[1,4,1024]{2,1,0:T(4,128)S(1)}, f32[1,4,1024]{2,1,0:T(4,128)}, u32[]{:S(2)}) copy-start(f32[1,4,1024]{2,1,0:T(4,128)} %param.23) | copy-start | bytes 49156
  145.1 18.8 %copy-start.22 = (bf16[1024]{0:T(1024)(128)(2,1)S(1)}, bf16[1024]{0:T(1024)(128)(2,1)}, u32[]{:S(2)}) copy-start(bf16[1024]{0:T(1024)(128)(2,1)} %gather_fusion.3) | copy-start | bytes 6148
  145.1 18.9 %copy-start.3 = (f32[1,16,128,128]{3,2,1,0:T(8,128)S(1)}, f32[1,16,128,128]{3,2,1,0:T(8,128)}, u32[]{:S(2)}) copy-start(f32[1,16,128,128]{3,2,1,0:T(8,128)} %get-tuple-element.70) | copy-start | bytes 3145732
  170.5 14.2 %copy-start.4 = (bf16[262144]{0:T(1024)(128)(2,1)}, bf16[262144]{0:T(1024)(128)(2,1)S(1)}, u32[]{:S(2)}) copy-start(bf16[262144]{0:T(1024)(128)(2,1)S(1)} %convert_element_type.608) | copy-start | bytes 1572868
  170.6 11.7 %copy-start.17 = (bf16[2,1,16,128,128]{4,3,2,1,0:T(8,128)(2,1)S(1)}, bf16[2,1,16,128,128]{4,3,2,1,0:T(8,128)(2,1)}, u32[]{:S(2)}) copy-start(bf16[2,1,16,128,128]{4,3,2,1,0:T(8,128)(2,1)} %param.18) | copy-start | bytes 3145732
  170.6 6.9 %collective-permute-start.10 = (bf16[1,4,128,128]{3,2,1,0:T(8,128)(2,1)S(1)}, bf16[1,4,128,128]{3,2,1,0:T(8,128)(2,1)S(1)}, u32[]{:S(2)}, u32[]{:S(2)}) collective-permute-start(bf16[1,4,128,128]{3,2,1,0:T(8,128)(2,1)S(1)} %get-tuple-element.76), channel_id=1, source_target_pairs={{0,1},{1,2},{2,3},{3,4},{4,5},{5,6},{6,7},{8,9},{9,10},{10,11},{11... | collective-permute-start | bytes 393224 | tf_op jit(solution)/shard_map/ppermute | solution.py:30
  175.6 6.6 %collective-permute-start.11 = (bf16[1,4,128,128]{3,2,1,0:T(8,128)(2,1)S(1)}, bf16[1,4,128,128]{3,2,1,0:T(8,128)(2,1)S(1)}, u32[]{:S(2)}, u32[]{:S(2)}) collective-permute-start(bf16[1,4,128,128]{3,2,1,0:T(8,128)(2,1)S(1)} %get-tuple-element.77), channel_id=1, source_target_pairs={{1,0},{2,1},{3,2},{4,3},{5,4},{6,5},{7,6},{9,8},{10,9},{11,10},{12... | collective-permute-start | bytes 393224 | tf_op jit(solution)/shard_map/ppermute | solution.py:32
  191.5 14.8 %copy-start.7 = (bf16[262144]{0:T(1024)(128)(2,1)}, bf16[262144]{0:T(1024)(128)(2,1)S(1)}, u32[]{:S(2)}) copy-start(bf16[262144]{0:T(1024)(128)(2,1)S(1)} %convert_element_type.609) | copy-start | bytes 1572868
  191.5 12.4 %copy-start.5 = (bf16[262144]{0:T(1024)(128)(2,1)S(1)}, bf16[262144]{0:T(1024)(128)(2,1)}, u32[]{:S(2)}) copy-start(bf16[262144]{0:T(1024)(128)(2,1)} %copy-done.4) | copy-start | bytes 1572868
  191.5 7.4 %collective-permute-start.12 = (bf16[1,4,128,128]{3,2,1,0:T(8,128)(2,1)S(1)}, bf16[1,4,128,128]{3,2,1,0:T(8,128)(2,1)S(1)}, u32[]{:S(2)}, u32[]{:S(2)}) collective-permute-start(bf16[1,4,128,128]{3,2,1,0:T(8,128)(2,1)S(1)} %get-tuple-element.74), channel_id=1, source_target_pairs={{0,1},{1,2},{2,3},{3,4},{4,5},{5,6},{6,7},{8,9},{9,10},{10,11},{11... | collective-permute-start | bytes 393224 | tf_op jit(solution)/shard_map/ppermute | solution.py:30
  197.0 6.7 %collective-permute-start.13 = (bf16[1,4,128,128]{3,2,1,0:T(8,128)(2,1)S(1)}, bf16[1,4,128,128]{3,2,1,0:T(8,128)(2,1)S(1)}, u32[]{:S(2)}, u32[]{:S(2)}) collective-permute-start(bf16[1,4,128,128]{3,2,1,0:T(8,128)(2,1)S(1)} %get-tuple-element.75), channel_id=1, source_target_pairs={{1,0},{2,1},{3,2},{4,3},{5,4},{6,5},{7,6},{9,8},{10,9},{11,10},{12... | collective-permute-start | bytes 393224 | tf_op jit(solution)/shard_map/ppermute | solution.py:32
  212.8 11.3 %copy-start.10 = (bf16[262144]{0:T(1024)(128)(2,1)}, bf16[262144]{0:T(1024)(128)(2,1)S(1)}, u32[]{:S(2)}) copy-start(bf16[262144]{0:T(1024)(128)(2,1)S(1)} %convert_element_type.610) | copy-start | bytes 1572868
  212.8 8.9 %copy-start.8 = (bf16[262144]{0:T(1024)(128)(2,1)S(1)}, bf16[262144]{0:T(1024)(128)(2,1)}, u32[]{:S(2)}) copy-start(bf16[262144]{0:T(1024)(128)(2,1)} %copy-done.7) | copy-start | bytes 1572868
  212.9 3.9 collective-permute-start.14
  214.8 6.8 %collective-permute-start.15 = (bf16[1,4,128,128]{3,2,1,0:T(8,128)(2,1)S(1)}, bf16[1,4,128,128]{3,2,1,0:T(8,128)(2,1)S(1)}, u32[]{:S(2)}, u32[]{:S(2)}) collective-permute-start(bf16[1,4,128,128]{3,2,1,0:T(8,128)(2,1)S(1)} %get-tuple-element.73), channel_id=1, source_target_pairs={{1,0},{2,1},{3,2},{4,3},{5,4},{6,5},{7,6},{9,8},{10,9},{11,10},{12... | collective-permute-start | bytes 393224 | tf_op jit(solution)/shard_map/ppermute | solution.py:32
  230.6 1.2 copy-start.6
  230.6 1.4 copy-start.9
  230.7 1.5 copy-start.11
  230.7 0.8 copy-start.13
  232.2 3.2 copy-start.12
Sparse Core Ops, SparseCore 0:
  235.5 294.2 all-reduce.10
where the time goes:
time: 547 us; the launch traced here: 539 us
  waiting for transfers between devices  314 us (57%)
  other arithmetic  109 us (20%)
  local copies, waits for them, and re-layouts  47.4 us (9%)
  starting transfers between devices  42.7 us (8%)
  between operations  25.6 us (5%)
    psum x1, waiting for transfers between devices, body(): summed = lax.psum(gradient, 'shot')  292 us
    convert_element_type x4, other arithmetic, body(): inject(updated, source_ids, wavelet[:, moment:moment + 1], anchor)  44.6 us
    gather x4, local copies, waits for them, and re-layouts, record(): jnp.take_along_axis(wavefield.reshape(shot_count, -1), flat_index, axis=1)  38.5 us
    ppermute x8, starting transfers between devices, padded_2(): lax.ppermute(tail, axis, [(i, (i + 1) % count) for i in range(ends)])  32.1 us
    unnamed x7, other arithmetic  26.2 us
    ppermute x8, waiting for transfers between devices, padded_2(): lax.ppermute(head, axis, [((i + 1) % count, i) for i in range(ends)])  20.1 us
    convert_element_type x4, other arithmetic, body(): images.append(laplacian.astype(jnp.bfloat16))  12.2 us
  transfers between devices with their start and end apart: 17, of which 9 were waited for; matrix products, arithmetic and copies ran while one was open for 16% of the time, Pallas kernels for 0%

commit v1 on v0

--- a/solution.py
+++ b/solution.py
@@ -3,8 +3,11 @@
 import jax
 import jax.numpy as jnp
 from jax import lax
+from jax.sharding import Mesh
 from jax.sharding import PartitionSpec as P
 
+SHOT = ("y", "zhi", "core")
+DEPTH = ("x", "zlo")
 CZ = 16
 NX = 128
 NY = 128
@@ -80,6 +83,34 @@
     return flattened.reshape(wavefield.shape)
 
 
+def cell_coords(cell_ids, anchor):
+    plane_size = NX * NY
+    planes = cell_ids // plane_size - anchor
+    rest = cell_ids % plane_size
+    return planes, rest // NY, rest % NY
+
+
+def inject_one(wavefield, cell_ids, values, anchor):
+    planes, rows, columns = cell_coords(cell_ids, anchor)
+    shape = wavefield.shape
+    hit = (
+        (lax.broadcasted_iota(jnp.int32, shape, 1) == planes[:, None, None, None])
+        & (lax.broadcasted_iota(jnp.int32, shape, 2) == rows[:, None, None, None])
+        & (lax.broadcasted_iota(jnp.int32, shape, 3) == columns[:, None, None, None])
+    )
+    return jnp.where(hit, wavefield + values[:, :, None, None], wavefield)
+
+
+def record_rows(wavefield, cell_ids, anchor):
+    depth_len = wavefield.shape[1]
+    planes, rows, columns = cell_coords(cell_ids, anchor)
+    row_ids = jnp.clip(planes, 0, depth_len - 1) * NX + rows
+    table = wavefield.reshape(-1, NY)
+    picked = table[row_ids[0]].astype(jnp.float32)
+    lanes = lax.broadcasted_iota(jnp.int32, picked.shape, 1)
+    return jnp.sum(jnp.where(lanes == columns[0][:, None], picked, 0.0), axis=1)[None]
+
+
 def record(wavefield, cell_ids, anchor):
     shot_count = wavefield.shape[0]
     plane_size = NX * NY
@@ -90,8 +121,34 @@
     )
 
 
+HALVINGS = (("core", 1), ("zhi", 1), ("zhi", 2), ("y", 1), ("y", 2))
+
+
+def partner_bit(axis, mask):
+    count = lax.axis_size(axis)
+    bit = (lax.axis_index(axis) // mask) % 2
+    return bit, [(i, i ^ mask) for i in range(count)]
+
+
+def reduce_shots(gradient):
+    rows = gradient.reshape(-1, gradient.shape[-1])
+    for axis, mask in HALVINGS:
+        bit, perm = partner_bit(axis, mask)
+        half = rows.shape[0] // 2
+        keep = lax.dynamic_slice_in_dim(rows, bit * half, half, 0)
+        send = lax.dynamic_slice_in_dim(rows, (1 - bit) * half, half, 0)
+        rows = keep + lax.ppermute(send, axis, perm)
+    for axis, mask in reversed(HALVINGS):
+        bit, perm = partner_bit(axis, mask)
+        other = lax.ppermute(rows, axis, perm)
+        rows = jnp.where(
+            bit == 0, jnp.concatenate([rows, other]), jnp.concatenate([other, rows])
+        )
+    return rows.reshape(gradient.shape)
+
+
 def body(forward_start, adjoint_end, velocity, source_cell, wavelet, receiver_cell, observed):
-    anchor = lax.axis_index("depth") * CZ
+    anchor = lax.axis_index(DEPTH) * CZ
     wave_model = (courant * velocity) ** 2
     source_ids = source_cell[:, None]
     images = []
@@ -99,23 +156,23 @@
     earlier = forward_start[0]
     current = forward_start[1]
     for moment in range(STEPS):
-        padded = padded_2(current, (("depth", 1),), 4)
+        padded = padded_2(current, ((DEPTH, 1),), 4)
         laplacian = laplace(padded.astype(jnp.float32))
         updated = (
             2.0 * current.astype(jnp.float32) - earlier.astype(jnp.float32) + wave_model * laplacian
         )
-        updated = inject(updated, source_ids, wavelet[:, moment : moment + 1], anchor).astype(
+        updated = inject_one(updated, source_cell, wavelet[:, moment : moment + 1], anchor).astype(
             jnp.bfloat16
         )
         images.append(laplacian.astype(jnp.bfloat16))
-        residuals.append(record(updated, receiver_cell, anchor) - observed[:, moment])
+        residuals.append(record_rows(updated, receiver_cell, anchor) - observed[:, moment])
         earlier, current = (current, updated)
     images = list(lax.optimization_barrier(tuple(images)))
     nearer = adjoint_end[0]
     farther = adjoint_end[1]
     gradient = jnp.zeros(velocity.shape, jnp.float32)
     for moment in reversed(range(STEPS)):
-        padded = padded_2(nearer, (("depth", 1),), 4)
+        padded = padded_2(nearer, ((DEPTH, 1),), 4)
         laplacian = laplace(padded.astype(jnp.float32))
         updated = (
             2.0 * nearer.astype(jnp.float32) - farther.astype(jnp.float32) + wave_model * laplacian
@@ -125,8 +182,8 @@
             updated.astype(jnp.float32) * images[moment].astype(jnp.float32), axis=0
         )
         farther, nearer = (nearer, updated)
-    step_scale = step_base / math.sqrt(forward_start.shape[1] * lax.axis_size("shot"))
-    summed = lax.psum(gradient, "shot")
+    step_scale = step_base / math.sqrt(forward_start.shape[1] * lax.axis_size(SHOT))
+    summed = reduce_shots(gradient)
     velocity_new = jnp.clip(velocity - step_scale * summed, low_speed, high_speed)
     forward_end = jnp.stack([earlier, current])
     adjoint_start = jnp.stack([nearer, farther])
@@ -134,23 +191,24 @@
 
 
 def solution(mesh):
+    fine = Mesh(mesh.devices.reshape(4, 4, 2, 4, 2), ("y", "zhi", "core", "x", "zlo"))
     placed = (
-        P(None, "shot", "depth", None, None),
-        P(None, "shot", "depth", None, None),
-        P("depth", None, None),
-        P("shot"),
-        P("shot", None),
-        P("shot", None),
-        P("shot", None, None),
+        P(None, SHOT, DEPTH, None, None),
+        P(None, SHOT, DEPTH, None, None),
+        P(DEPTH, None, None),
+        P(SHOT),
+        P(SHOT, None),
+        P(SHOT, None),
+        P(SHOT, None, None),
     )
     return jax.shard_map(
         body,
-        mesh=mesh,
+        mesh=fine,
         in_specs=placed,
         out_specs=(
-            P(None, "shot", "depth", None, None),
-            P(None, "shot", "depth", None, None),
-            P("depth", None, None),
+            P(None, SHOT, DEPTH, None, None),
+            P(None, SHOT, DEPTH, None, None),
+            P(DEPTH, None, None),
         ),
         check_vma=False,
     )

time: 547 us -> 243 us (0.44); the launches traced: 539 us -> 242 us
  waiting for transfers between devices: 314 us -> 63.4 us
  starting transfers between devices: 42.7 us -> 83.4 us
  other arithmetic: 109 us -> 70.6 us
  local copies, waits for them, and re-layouts: 47.4 us -> 22 us
  between operations: 25.6 us -> 2.18 us
    psum x1 -> x0, waiting for transfers between devices: 292 us -> none  [body(): summed = lax.psum(gradient, 'shot')]
    ppermute x0 -> x10, starting transfers between devices: none -> 40.9 us  [the longest x5 21 us: reduce_shots(): other = lax.ppermute(rows, axis, perm)]
    convert_element_type x4, other arithmetic: 44.6 us -> 4.46 us  [body(): inject_one(updated, source_cell, wavelet[:, moment:moment + 1], anchor)]
    ppermute x0 -> x10, waiting for transfers between devices: none -> 37.8 us  [the longest x5 19.6 us: reduce_shots(): rows = keep + lax.ppermute(send, axis, perm)]
    gather x4, local copies, waits for them, and re-layouts: 38.5 us -> 16 us  [record_rows(): picked = table[row_ids[0]].astype(jnp.float32)]
  transfers between devices with their start and end apart: 17 -> 26, of which waited for: 9 -> 20; matrix products, arithmetic and copies ran while one was open for 16% -> 11% of each run, Pallas kernels for 0% -> 0%
where the time goes in v1:
time: 243 us; the launch traced here: 242 us
  starting transfers between devices  83.4 us (34%)
  other arithmetic  70.6 us (29%)
  waiting for transfers between devices  63.4 us (26%)
  local copies, waits for them, and re-layouts  22 us (9%)
    ppermute x8, starting transfers between devices, padded_2(): lax.ppermute(tail, axis, [(i, (i + 1) % count) for i in range(ends)])  32.1 us
    unnamed x7, other arithmetic  26.2 us
    ppermute x8, waiting for transfers between devices, padded_2(): lax.ppermute(head, axis, [((i + 1) % count, i) for i in range(ends)])  22.7 us
    ppermute x5, starting transfers between devices, reduce_shots(): other = lax.ppermute(rows, axis, perm)  21 us
    ppermute x5, starting transfers between devices, reduce_shots(): rows = keep + lax.ppermute(send, axis, perm)  20 us
    ppermute x5, waiting for transfers between devices, reduce_shots(): rows = keep + lax.ppermute(send, axis, perm)  19.6 us
    ppermute x5, waiting for transfers between devices, reduce_shots(): other = lax.ppermute(rows, axis, perm)  18.2 us
    gather x4, local copies, waits for them, and re-layouts, record_rows(): picked = table[row_ids[0]].astype(jnp.float32)  16 us
  transfers between devices with their start and end apart: 26, of which 20 were waited for; matrix products, arithmetic and copies ran while one was open for 11% of the time, Pallas kernels for 0%

profile of v1, /device:TPU:1, one launch (start us, length us, event | category | flops | bytes accessed | tf_op | source)
XLA Modules:
  0.0 241.6 jit_solution(13976629649753980906)
XLA Ops:
  0.7 1.2 slice_bitcast_fusion.1
  1.9 4.4 %collective-permute-start = (bf16[1,4,128,128]{3,2,1,0:T(8,128)(2,1)S(1)}, bf16[1,4,128,128]{3,2,1,0:T(8,128)(2,1)S(1)}, u32[]{:S(2)}, u32[]{:S(2)}) collective-permute-start(bf16[1,4,128,128]{3,2,1,0:T(8,128)(2,1)S(1)} %get-tuple-element.42), channel_id=1, source_target_pairs={{0,1},{1,2},{2,3},{3,4},{4,5},{5,6},{6,7},{8,9},{9,10},{10,11},{11... | collective-permute-start | bytes 393224 | tf_op jit(solution)/shard_map/ppermute | solution.py:33
  6.3 1.3 collective-permute-start.1
  7.7 4.0 %collective-permute-start.8 = (bf16[1,4,128,128]{3,2,1,0:T(8,128)(2,1)S(1)}, bf16[1,4,128,128]{3,2,1,0:T(8,128)(2,1)S(1)}, u32[]{:S(2)}, u32[]{:S(2)}) collective-permute-start(bf16[1,4,128,128]{3,2,1,0:T(8,128)(2,1)S(1)} %get-tuple-element.34), channel_id=1, source_target_pairs={{0,1},{1,2},{2,3},{3,4},{4,5},{5,6},{6,7},{8,9},{9,10},{10,11},{11... | collective-permute-start | bytes 393224 | tf_op jit(solution)/shard_map/ppermute | solution.py:33
  11.7 1.3 collective-permute-start.9
  14.9 3.0 %fusion.229 = (bf16[1,16,128,128]{3,2,1,0:T(8,128)(2,1)}, f32[1,16,128,128]{3,2,1,0:T(8,128)S(1)}) fusion(f32[1,24,128,128]{3,2,1,0:T(8,128)S(1)} %maximum_convert_fusion), kind=kLoop, calls=%fused_computation.485 | loop fusion | flops 7864320 | bytes 12582912 | tf_op jit(solution)/shard_map/convert_element_type | solution.py:167
  19.0 4.2 %collective-permute-start.2 = (bf16[1,4,128,128]{3,2,1,0:T(8,128)(2,1)S(1)}, bf16[1,4,128,128]{3,2,1,0:T(8,128)(2,1)S(1)}, u32[]{:S(2)}, u32[]{:S(2)}) collective-permute-start(bf16[1,4,128,128]{3,2,1,0:T(8,128)(2,1)S(1)} %get-tuple-element.40), channel_id=1, source_target_pairs={{0,1},{1,2},{2,3},{3,4},{4,5},{5,6},{6,7},{8,9},{9,10},{10,11},{11... | collective-permute-start | bytes 393224 | tf_op jit(solution)/shard_map/ppermute | solution.py:33
  23.2 1.3 collective-permute-start.3
  25.2 5.8 %collective-permute-done.3 = bf16[1,4,128,128]{3,2,1,0:T(8,128)(2,1)S(1)} collective-permute-done((bf16[1,4,128,128]{3,2,1,0:T(8,128)(2,1)S(1)}, bf16[1,4,128,128]{3,2,1,0:T(8,128)(2,1)S(1)}, u32[]{:S(2)}, u32[]{:S(2)}) %collective-permute-start.3) | collective-permute-done | bytes 131104 | tf_op jit(solution)/shard_map/ppermute | solution.py:35
  31.1 3.0 %fusion.227 = (bf16[1,16,128,128]{3,2,1,0:T(8,128)(2,1)}, f32[1,16,128,128]{3,2,1,0:T(8,128)S(1)}) fusion(f32[1,24,128,128]{3,2,1,0:T(8,128)S(1)} %maximum_convert_fusion.1), kind=kLoop, calls=%fused_computation.484 | loop fusion | flops 7864320 | bytes 12582912 | tf_op jit(solution)/shard_map/convert_element_type | solution.py:167
  35.2 3.2 %collective-permute-start.4 = (bf16[1,4,128,128]{3,2,1,0:T(8,128)(2,1)S(1)}, bf16[1,4,128,128]{3,2,1,0:T(8,128)(2,1)S(1)}, u32[]{:S(2)}, u32[]{:S(2)}) collective-permute-start(bf16[1,4,128,128]{3,2,1,0:T(8,128)(2,1)S(1)} %get-tuple-element.38), channel_id=1, source_target_pairs={{0,1},{1,2},{2,3},{3,4},{4,5},{5,6},{6,7},{8,9},{9,10},{10,11},{11... | collective-permute-start | bytes 393224 | tf_op jit(solution)/shard_map/ppermute | solution.py:33
  38.4 1.3 collective-permute-start.5
  40.4 4.6 %collective-permute-done.5 = bf16[1,4,128,128]{3,2,1,0:T(8,128)(2,1)S(1)} collective-permute-done((bf16[1,4,128,128]{3,2,1,0:T(8,128)(2,1)S(1)}, bf16[1,4,128,128]{3,2,1,0:T(8,128)(2,1)S(1)}, u32[]{:S(2)}, u32[]{:S(2)}) %collective-permute-start.5) | collective-permute-done | bytes 131104 | tf_op jit(solution)/shard_map/ppermute | solution.py:35
  45.1 3.1 %fusion.225 = (bf16[1,16,128,128]{3,2,1,0:T(8,128)(2,1)}, f32[1,16,128,128]{3,2,1,0:T(8,128)S(1)}) fusion(f32[1,24,128,128]{3,2,1,0:T(8,128)S(1)} %maximum_convert_fusion.2), kind=kLoop, calls=%fused_computation.483 | loop fusion | flops 7864320 | bytes 12582912 | tf_op jit(solution)/shard_map/convert_element_type | solution.py:167
  48.1 1.2 fusion.12
  49.3 4.4 %collective-permute-start.6 = (bf16[1,4,128,128]{3,2,1,0:T(8,128)(2,1)S(1)}, bf16[1,4,128,128]{3,2,1,0:T(8,128)(2,1)S(1)}, u32[]{:S(2)}, u32[]{:S(2)}) collective-permute-start(bf16[1,4,128,128]{3,2,1,0:T(8,128)(2,1)S(1)} %get-tuple-element.36), channel_id=1, source_target_pairs={{0,1},{1,2},{2,3},{3,4},{4,5},{5,6},{6,7},{8,9},{9,10},{10,11},{11... | collective-permute-start | bytes 393224 | tf_op jit(solution)/shard_map/ppermute | solution.py:33
  53.8 1.3 collective-permute-start.7
  55.1 3.2 %fusion.6 = f32[1,16,128,128]{3,2,1,0:T(8,128)} fusion(f32[1,24,128,128]{3,2,1,0:T(8,128)S(1)} %maximum_convert_fusion.4, bf16[2,1,16,128,128]{4,3,2,1,0:T(8,128)(2,1)S(1)} %copy-done.14, f32[16,128,128]{2,1,0:T(8,128)S(1)} %copy-done), kind=kLoop, calls=%fused_computation.162 | loop fusion | flops 9699328 | bytes 14155776 | tf_op jit(solution)/shard_map/add | solution.py:178
  58.3 3.2 %gather_fusion.3 = bf16[1024,128]{1,0:T(8,128)(2,1)S(1)} fusion(bf16[2048,128]{1,0:T(8,128)(2,1)S(1)} %bitcast.92, s32[1024]{0:T(1024)S(1)} %broadcast_clamp_fusion), kind=kCustom, calls=%fused_computation.3 | custom fusion | bytes 528384 | tf_op jit(solution)/shard_map/gather | solution.py:109
  61.5 4.3 %gather_fusion.2 = bf16[1024,128]{1,0:T(8,128)(2,1)} fusion(bf16[2048,128]{1,0:T(8,128)(2,1)S(1)} %bitcast.93, s32[1024]{0:T(1024)S(1)} %broadcast_clamp_fusion), kind=kCustom, calls=%fused_computation.2 | custom fusion | bytes 528384 | tf_op jit(solution)/shard_map/gather | solution.py:109
  65.7 4.3 %gather_fusion.1 = bf16[1024,128]{1,0:T(8,128)(2,1)} fusion(bf16[2048,128]{1,0:T(8,128)(2,1)S(1)} %bitcast.94, s32[1024]{0:T(1024)S(1)} %broadcast_clamp_fusion), kind=kCustom, calls=%fused_computation.1 | custom fusion | bytes 528384 | tf_op jit(solution)/shard_map/gather | solution.py:109
  70.1 3.0 %fusion.223 = (bf16[1,16,128,128]{3,2,1,0:T(8,128)(2,1)}, f32[1,16,128,128]{3,2,1,0:T(8,128)S(1)}) fusion(f32[1,24,128,128]{3,2,1,0:T(8,128)S(1)} %maximum_convert_fusion.3), kind=kLoop, calls=%fused_computation.482 | loop fusion | flops 7864320 | bytes 12582912 | tf_op jit(solution)/shard_map/convert_element_type | solution.py:167
  74.3 4.3 %gather_fusion = bf16[1024,128]{1,0:T(8,128)(2,1)} fusion(bf16[2048,128]{1,0:T(8,128)(2,1)S(1)} %bitcast.100, s32[1024]{0:T(1024)S(1)} %broadcast_clamp_fusion), kind=kCustom, calls=%fused_computation | custom fusion | bytes 528384 | tf_op jit(solution)/shard_map/gather | solution.py:109
  78.6 1.7 select_reduce_fusion
  80.3 6.6 %scatter_fusion = f32[262144]{0:T(1024)S(1)} fusion(f32[262144]{0:T(1024)S(1)} %bitcast.96, s32[1024]{0:T(1024)S(1)} %broadcast_select_fusion, f32[1024]{0:T(1024)S(1)} %bitcast.125), kind=kCustom, calls=%fused_computation.4 | custom fusion | flops 1024 | bytes 16384
  87.1 4.1 %collective-permute-start.10 = (bf16[1,4,128,128]{3,2,1,0:T(8,128)(2,1)S(1)}, bf16[1,4,128,128]{3,2,1,0:T(8,128)(2,1)S(1)}, u32[]{:S(2)}, u32[]{:S(2)}) collective-permute-start(bf16[1,4,128,128]{3,2,1,0:T(8,128)(2,1)S(1)} %get-tuple-element.32), channel_id=1, source_target_pairs={{0,1},{1,2},{2,3},{3,4},{4,5},{5,6},{6,7},{8,9},{9,10},{10,11},{11... | collective-permute-start | bytes 393224 | tf_op jit(solution)/shard_map/ppermute | solution.py:33
  91.2 1.3 collective-permute-start.11
  93.2 3.8 %collective-permute-done.11 = bf16[1,4,128,128]{3,2,1,0:T(8,128)(2,1)S(1)} collective-permute-done((bf16[1,4,128,128]{3,2,1,0:T(8,128)(2,1)S(1)}, bf16[1,4,128,128]{3,2,1,0:T(8,128)(2,1)S(1)}, u32[]{:S(2)}, u32[]{:S(2)}) %collective-permute-start.11) | collective-permute-done | bytes 131104 | tf_op jit(solution)/shard_map/ppermute | solution.py:35
  97.1 2.4 fusion.7
  99.5 6.5 %scatter_fusion.1 = f32[262144]{0:T(1024)S(1)} fusion(f32[262144]{0:T(1024)S(1)} %bitcast.98, s32[1024]{0:T(1024)S(1)} %broadcast_select_fusion, f32[1024]{0:T(1024)S(1)} %bitcast.124), kind=kCustom, calls=%fused_computation.5 | custom fusion | flops 1024 | bytes 16384
  106.1 5.6 %collective-permute-start.12 = (bf16[1,4,128,128]{3,2,1,0:T(8,128)(2,1)S(1)}, bf16[1,4,128,128]{3,2,1,0:T(8,128)(2,1)S(1)}, u32[]{:S(2)}, u32[]{:S(2)}) collective-permute-start(bf16[1,4,128,128]{3,2,1,0:T(8,128)(2,1)S(1)} %get-tuple-element.30), channel_id=1, source_target_pairs={{0,1},{1,2},{2,3},{3,4},{4,5},{5,6},{6,7},{8,9},{9,10},{10,11},{11... | collective-permute-start | bytes 393224 | tf_op jit(solution)/shard_map/ppermute | solution.py:33
  111.7 1.3 collective-permute-start.13
  113.7 4.5 %collective-permute-done.13 = bf16[1,4,128,128]{3,2,1,0:T(8,128)(2,1)S(1)} collective-permute-done((bf16[1,4,128,128]{3,2,1,0:T(8,128)(2,1)S(1)}, bf16[1,4,128,128]{3,2,1,0:T(8,128)(2,1)S(1)}, u32[]{:S(2)}, u32[]{:S(2)}) %collective-permute-start.13) | collective-permute-done | bytes 131104 | tf_op jit(solution)/shard_map/ppermute | solution.py:35
  118.3 2.4 fusion.14
  120.7 6.5 %scatter_fusion.2 = f32[262144]{0:T(1024)S(1)} fusion(f32[262144]{0:T(1024)S(1)} %bitcast.99, s32[1024]{0:T(1024)S(1)} %broadcast_select_fusion, f32[1024]{0:T(1024)S(1)} %bitcast.123), kind=kCustom, calls=%fused_computation.6 | custom fusion | flops 1024 | bytes 16384
  128.0 2.1 collective-permute-start.14
  130.2 1.3 collective-permute-start.15
  132.1 4.1 %collective-permute-done.15 = bf16[1,4,128,128]{3,2,1,0:T(8,128)(2,1)S(1)} collective-permute-done((bf16[1,4,128,128]{3,2,1,0:T(8,128)(2,1)S(1)}, bf16[1,4,128,128]{3,2,1,0:T(8,128)(2,1)S(1)}, u32[]{:S(2)}, u32[]{:S(2)}) %collective-permute-start.15) | collective-permute-done | bytes 131104 | tf_op jit(solution)/shard_map/ppermute | solution.py:35
  136.2 1.2 maximum_convert_fusion.7
  137.4 3.3 %fusion.16 = f32[1,16,128,128]{3,2,1,0:T(8,128)S(1)} fusion(bf16[1,16,128,128]{3,2,1,0:T(8,128)(2,1)} %bitcast.110, bf16[1,16,128,128]{3,2,1,0:T(8,128)(2,1)S(1)} %bitcast.114, f32[1,24,128,128]{3,2,1,0:T(8,128)S(1)} %maximum_convert_fusion.7, f32[16,128,128]{2,1,0:T(8,128)S(1)} %copy-done), kind=kLoop, calls=%fused_computation.172 | loop fusion | flops 9699328 | bytes 14155776 | tf_op jit(solution)/shard_map/add | solution.py:178
  140.7 6.5 %scatter_fusion.3 = f32[262144]{0:T(1024)S(1)} fusion(f32[262144]{0:T(1024)S(1)} %bitcast.97, s32[1024]{0:T(1024)S(1)} %broadcast_select_fusion, f32[1024]{0:T(1024)S(1)} %bitcast.122), kind=kCustom, calls=%fused_computation.7 | custom fusion | flops 1024 | bytes 16384
  148.7 2.1 fusion.9
  151.7 6.2 %collective-permute-start.16 = (f32[1024,128]{1,0:T(8,128)}, f32[1024,128]{1,0:T(8,128)}, u32[]{:S(2)}, u32[]{:S(2)}) collective-permute-start(f32[1024,128]{1,0:T(8,128)} %constant_dynamic-slice_fusion.4), channel_id=1, source_target_pairs={{0,8},{8,0},{1,9},{9,1},{2,10},{10,2},{3,11},{11,3},{4,12},{12,4},... | collective-permute-start | bytes 1572872 | tf_op jit(solution)/shard_map/ppermute | solution.py:140
  157.9 1.9 collective-permute-done.16
  161.7 3.1 %collective-permute-start.17 = (f32[512,128]{1,0:T(8,128)S(1)}, f32[512,128]{1,0:T(8,128)S(1)}, u32[]{:S(2)}, u32[]{:S(2)}) collective-permute-start(f32[512,128]{1,0:T(8,128)S(1)} %constant_dynamic-slice_fusion.3), channel_id=1, source_target_pairs={{0,16},{16,0},{32,48},{48,32},{1,17},{17,1},{33,49},{49,33},{2,18}... | collective-permute-start | bytes 786440 | tf_op jit(solution)/shard_map/ppermute | solution.py:140
  164.8 11.9 %collective-permute-done.17 = f32[512,128]{1,0:T(8,128)S(1)} collective-permute-done((f32[512,128]{1,0:T(8,128)S(1)}, f32[512,128]{1,0:T(8,128)S(1)}, u32[]{:S(2)}, u32[]{:S(2)}) %collective-permute-start.17) | collective-permute-done | bytes 262176 | tf_op jit(solution)/shard_map/ppermute | solution.py:140
  177.7 6.3 %collective-permute-start.18 = (f32[256,128]{1,0:T(8,128)S(1)}, f32[256,128]{1,0:T(8,128)}, u32[]{:S(2)}, u32[]{:S(2)}) collective-permute-start(f32[256,128]{1,0:T(8,128)S(1)} %constant_dynamic-slice_fusion.2), channel_id=1, source_target_pairs={{0,32},{16,48},{32,0},{48,16},{1,33},{17,49},{33,1},{49,17},{2,34}... | collective-permute-start | bytes 393224 | tf_op jit(solution)/shard_map/ppermute | solution.py:140
  184.0 2.5 %collective-permute-done.18 = f32[256,128]{1,0:T(8,128)} collective-permute-done((f32[256,128]{1,0:T(8,128)S(1)}, f32[256,128]{1,0:T(8,128)}, u32[]{:S(2)}, u32[]{:S(2)}) %collective-permute-start.18) | collective-permute-done | bytes 131104 | tf_op jit(solution)/shard_map/ppermute | solution.py:140
  187.5 1.4 collective-permute-start.19
  188.8 2.0 collective-permute-done.19
  190.9 3.0 %collective-permute-start.20 = (f32[64,128]{1,0:T(8,128)S(1)}, f32[64,128]{1,0:T(8,128)S(1)}, u32[]{:S(2)}, u32[]{:S(2)}) collective-permute-start(f32[64,128]{1,0:T(8,128)S(1)} %constant_dynamic-slice_fusion), channel_id=1, source_target_pairs={{0,128},{64,192},{128,0},{192,64},{1,129},{65,193},{129,1},{193,65... | collective-permute-start | bytes 98312 | tf_op jit(solution)/shard_map/ppermute | solution.py:140
  193.9 1.4 collective-permute-done.20
  195.2 3.1 %collective-permute-start.21 = (f32[64,128]{1,0:T(8,128)S(1)}, f32[64,128]{1,0:T(8,128)S(1)}, u32[]{:S(2)}, u32[]{:S(2)}) collective-permute-start(f32[64,128]{1,0:T(8,128)S(1)} %dynamic-slice_add_fusion.4), channel_id=1, source_target_pairs={{0,128},{64,192},{128,0},{192,64},{1,129},{65,193},{129,1},{193,65... | collective-permute-start | bytes 98312 | tf_op jit(solution)/shard_map/ppermute | solution.py:143
  198.4 1.3 collective-permute-done.21
  199.7 1.2 collective-permute-start.22
  200.9 2.0 collective-permute-done.22
  202.9 5.2 %collective-permute-start.23 = (f32[256,128]{1,0:T(8,128)S(1)}, f32[256,128]{1,0:T(8,128)}, u32[]{:S(2)}, u32[]{:S(2)}) collective-permute-start(f32[256,128]{1,0:T(8,128)S(1)} %maximum_select_fusion.3), channel_id=1, source_target_pairs={{0,32},{16,48},{32,0},{48,16},{1,33},{17,49},{33,1},{49,17},{2,34}... | collective-permute-start | bytes 393224 | tf_op jit(solution)/shard_map/ppermute | solution.py:143
  208.1 2.7 %collective-permute-done.23 = f32[256,128]{1,0:T(8,128)} collective-permute-done((f32[256,128]{1,0:T(8,128)S(1)}, f32[256,128]{1,0:T(8,128)}, u32[]{:S(2)}, u32[]{:S(2)}) %collective-permute-start.23) | collective-permute-done | bytes 131104 | tf_op jit(solution)/shard_map/ppermute | solution.py:143
  211.9 11.8 %collective-permute-done.24 = f32[512,128]{1,0:T(8,128)} collective-permute-done((f32[512,128]{1,0:T(8,128)S(1)}, f32[512,128]{1,0:T(8,128)}, u32[]{:S(2)}, u32[]{:S(2)}) %collective-permute-start.24) | collective-permute-done | bytes 262176 | tf_op jit(solution)/shard_map/ppermute | solution.py:143
  223.8 1.9 maximum_select_fusion.1
  225.6 11.3 %collective-permute-start.25 = (f32[1024,128]{1,0:T(8,128)}, f32[1024,128]{1,0:T(8,128)}, u32[]{:S(2)}, u32[]{:S(2)}) collective-permute-start(f32[1024,128]{1,0:T(8,128)} %maximum_select_fusion.1), channel_id=1, source_target_pairs={{0,8},{8,0},{1,9},{9,1},{2,10},{10,2},{3,11},{11,3},{4,12},{12,4},... | collective-permute-start | bytes 1572872 | tf_op jit(solution)/shard_map/ppermute | solution.py:143
  237.0 1.5 pad_maximum_fusion
  238.8 1.7 fusion.213
  240.5 1.1 subtract_clamp_fusion
  (104 shorter events, 17.0 us)
Async XLA Ops:
  0.6 12.5 %copy-start.21 = (s32[2]{0:T(128)S(1)}, s32[2]{0:T(128)}, u32[]{:S(2)}) copy-start(s32[2]{0:T(128)} %constant.355) | copy-start | bytes 28
  0.6 12.6 %copy-start.22 = (s32[2]{0:T(128)S(1)}, s32[2]{0:T(128)}, u32[]{:S(2)}) copy-start(s32[2]{0:T(128)} %constant.358) | copy-start | bytes 28
  0.7 6.9 %copy-start.13 = (bf16[2,1,16,128,128]{4,3,2,1,0:T(8,128)(2,1)S(1)}, bf16[2,1,16,128,128]{4,3,2,1,0:T(8,128)(2,1)}, u32[]{:S(2)}) copy-start(bf16[2,1,16,128,128]{4,3,2,1,0:T(8,128)(2,1)} %param.8) | copy-start | bytes 3145732
  0.7 12.3 %copy-start.19 = (s32[1,1024]{1,0:T(1,128)S(1)}, s32[1,1024]{1,0:T(1,128)}, u32[]{:S(2)}) copy-start(s32[1,1024]{1,0:T(1,128)} %param.12) | copy-start | bytes 12292
  0.7 13.3 %copy-start.20 = (f32[1,4]{1,0:T(1,128)S(1)}, f32[1,4]{1,0:T(1,128)}, u32[]{:S(2)}) copy-start(f32[1,4]{1,0:T(1,128)} %param.11) | copy-start | bytes 52
  1.9 12.8 %collective-permute-start = (bf16[1,4,128,128]{3,2,1,0:T(8,128)(2,1)S(1)}, bf16[1,4,128,128]{3,2,1,0:T(8,128)(2,1)S(1)}, u32[]{:S(2)}, u32[]{:S(2)}) collective-permute-start(bf16[1,4,128,128]{3,2,1,0:T(8,128)(2,1)S(1)} %get-tuple-element.42), channel_id=1, source_target_pairs={{0,1},{1,2},{2,3},{3,4},{4,5},{5,6},{6,7},{8,9},{9,10},{10,11},{11... | collective-permute-start | bytes 393224 | tf_op jit(solution)/shard_map/ppermute | solution.py:33
  6.3 8.4 %collective-permute-start.1 = (bf16[1,4,128,128]{3,2,1,0:T(8,128)(2,1)S(1)}, bf16[1,4,128,128]{3,2,1,0:T(8,128)(2,1)S(1)}, u32[]{:S(2)}, u32[]{:S(2)}) collective-permute-start(bf16[1,4,128,128]{3,2,1,0:T(8,128)(2,1)S(1)} %get-tuple-element.43), channel_id=1, source_target_pairs={{1,0},{2,1},{3,2},{4,3},{5,4},{6,5},{7,6},{9,8},{10,9},{11,10},{12... | collective-permute-start | bytes 393224 | tf_op jit(solution)/shard_map/ppermute | solution.py:35
  7.7 32.1 %collective-permute-start.8 = (bf16[1,4,128,128]{3,2,1,0:T(8,128)(2,1)S(1)}, bf16[1,4,128,128]{3,2,1,0:T(8,128)(2,1)S(1)}, u32[]{:S(2)}, u32[]{:S(2)}) collective-permute-start(bf16[1,4,128,128]{3,2,1,0:T(8,128)(2,1)S(1)} %get-tuple-element.34), channel_id=1, source_target_pairs={{0,1},{1,2},{2,3},{3,4},{4,5},{5,6},{6,7},{8,9},{9,10},{10,11},{11... | collective-permute-start | bytes 393224 | tf_op jit(solution)/shard_map/ppermute | solution.py:33
  11.7 28.1 %collective-permute-start.9 = (bf16[1,4,128,128]{3,2,1,0:T(8,128)(2,1)S(1)}, bf16[1,4,128,128]{3,2,1,0:T(8,128)(2,1)S(1)}, u32[]{:S(2)}, u32[]{:S(2)}) collective-permute-start(bf16[1,4,128,128]{3,2,1,0:T(8,128)(2,1)S(1)} %get-tuple-element.35), channel_id=1, source_target_pairs={{1,0},{2,1},{3,2},{4,3},{5,4},{6,5},{7,6},{9,8},{10,9},{11,10},{12... | collective-permute-start | bytes 393224 | tf_op jit(solution)/shard_map/ppermute | solution.py:35
  14.8 3.1 %copy-start = (f32[16,128,128]{2,1,0:T(8,128)S(1)}, f32[16,128,128]{2,1,0:T(8,128)}, u32[]{:S(2)}) copy-start(f32[16,128,128]{2,1,0:T(8,128)} %param.9) | copy-start | bytes 3145732
  14.8 3.1 %copy-start.16 = (bf16[2,1,16,128,128]{4,3,2,1,0:T(8,128)(2,1)S(1)}, bf16[2,1,16,128,128]{4,3,2,1,0:T(8,128)(2,1)}, u32[]{:S(2)}) copy-start(bf16[2,1,16,128,128]{4,3,2,1,0:T(8,128)(2,1)} %param.7) | copy-start | bytes 3145732
  19.0 6.1 %collective-permute-start.2 = (bf16[1,4,128,128]{3,2,1,0:T(8,128)(2,1)S(1)}, bf16[1,4,128,128]{3,2,1,0:T(8,128)(2,1)S(1)}, u32[]{:S(2)}, u32[]{:S(2)}) collective-permute-start(bf16[1,4,128,128]{3,2,1,0:T(8,128)(2,1)S(1)} %get-tuple-element.40), channel_id=1, source_target_pairs={{0,1},{1,2},{2,3},{3,4},{4,5},{5,6},{6,7},{8,9},{9,10},{10,11},{11... | collective-permute-start | bytes 393224 | tf_op jit(solution)/shard_map/ppermute | solution.py:33
  23.2 7.7 %collective-permute-start.3 = (bf16[1,4,128,128]{3,2,1,0:T(8,128)(2,1)S(1)}, bf16[1,4,128,128]{3,2,1,0:T(8,128)(2,1)S(1)}, u32[]{:S(2)}, u32[]{:S(2)}) collective-permute-start(bf16[1,4,128,128]{3,2,1,0:T(8,128)(2,1)S(1)} %get-tuple-element.41), channel_id=1, source_target_pairs={{1,0},{2,1},{3,2},{4,3},{5,4},{6,5},{7,6},{9,8},{10,9},{11,10},{12... | collective-permute-start | bytes 393224 | tf_op jit(solution)/shard_map/ppermute | solution.py:35
  35.2 5.1 %collective-permute-start.4 = (bf16[1,4,128,128]{3,2,1,0:T(8,128)(2,1)S(1)}, bf16[1,4,128,128]{3,2,1,0:T(8,128)(2,1)S(1)}, u32[]{:S(2)}, u32[]{:S(2)}) collective-permute-start(bf16[1,4,128,128]{3,2,1,0:T(8,128)(2,1)S(1)} %get-tuple-element.38), channel_id=1, source_target_pairs={{0,1},{1,2},{2,3},{3,4},{4,5},{5,6},{6,7},{8,9},{9,10},{10,11},{11... | collective-permute-start | bytes 393224 | tf_op jit(solution)/shard_map/ppermute | solution.py:33
  38.4 6.5 %collective-permute-start.5 = (bf16[1,4,128,128]{3,2,1,0:T(8,128)(2,1)S(1)}, bf16[1,4,128,128]{3,2,1,0:T(8,128)(2,1)S(1)}, u32[]{:S(2)}, u32[]{:S(2)}) collective-permute-start(bf16[1,4,128,128]{3,2,1,0:T(8,128)(2,1)S(1)} %get-tuple-element.39), channel_id=1, source_target_pairs={{1,0},{2,1},{3,2},{4,3},{5,4},{6,5},{7,6},{9,8},{10,9},{11,10},{12... | collective-permute-start | bytes 393224 | tf_op jit(solution)/shard_map/ppermute | solution.py:35
  48.1 7.0 %copy-start.14 = (bf16[2,1,16,128,128]{4,3,2,1,0:T(8,128)(2,1)S(1)}, bf16[2,1,16,128,128]{4,3,2,1,0:T(8,128)(2,1)}, u32[]{:S(2)}) copy-start(bf16[2,1,16,128,128]{4,3,2,1,0:T(8,128)(2,1)} %param.8) | copy-start | bytes 3145732
  49.3 20.7 %collective-permute-start.6 = (bf16[1,4,128,128]{3,2,1,0:T(8,128)(2,1)S(1)}, bf16[1,4,128,128]{3,2,1,0:T(8,128)(2,1)S(1)}, u32[]{:S(2)}, u32[]{:S(2)}) collective-permute-start(bf16[1,4,128,128]{3,2,1,0:T(8,128)(2,1)S(1)} %get-tuple-element.36), channel_id=1, source_target_pairs={{0,1},{1,2},{2,3},{3,4},{4,5},{5,6},{6,7},{8,9},{9,10},{10,11},{11... | collective-permute-start | bytes 393224 | tf_op jit(solution)/shard_map/ppermute | solution.py:33
  53.8 16.2 %collective-permute-start.7 = (bf16[1,4,128,128]{3,2,1,0:T(8,128)(2,1)S(1)}, bf16[1,4,128,128]{3,2,1,0:T(8,128)(2,1)S(1)}, u32[]{:S(2)}, u32[]{:S(2)}) collective-permute-start(bf16[1,4,128,128]{3,2,1,0:T(8,128)(2,1)S(1)} %get-tuple-element.37), channel_id=1, source_target_pairs={{1,0},{2,1},{3,2},{4,3},{5,4},{6,5},{7,6},{9,8},{10,9},{11,10},{12... | collective-permute-start | bytes 393224 | tf_op jit(solution)/shard_map/ppermute | solution.py:35
  74.3 6.0 %copy-start.18 = (f32[1,4,1024]{2,1,0:T(4,128)S(1)}, f32[1,4,1024]{2,1,0:T(4,128)}, u32[]{:S(2)}) copy-start(f32[1,4,1024]{2,1,0:T(4,128)} %param.13) | copy-start | bytes 49156
  74.3 6.0 %copy-start.1 = (f32[1,16,128,128]{3,2,1,0:T(8,128)S(1)}, f32[1,16,128,128]{3,2,1,0:T(8,128)}, u32[]{:S(2)}) copy-start(f32[1,16,128,128]{3,2,1,0:T(8,128)} %fusion.6) | copy-start | bytes 3145732
  87.0 12.4 %copy-start.2 = (bf16[262144]{0:T(1024)(128)(2,1)}, bf16[262144]{0:T(1024)(128)(2,1)S(1)}, u32[]{:S(2)}) copy-start(bf16[262144]{0:T(1024)(128)(2,1)S(1)} %convert_element_type.468) | copy-start | bytes 1572868
  87.1 10.0 %copy-start.15 = (bf16[2,1,16,128,128]{4,3,2,1,0:T(8,128)(2,1)S(1)}, bf16[2,1,16,128,128]{4,3,2,1,0:T(8,128)(2,1)}, u32[]{:S(2)}) copy-start(bf16[2,1,16,128,128]{4,3,2,1,0:T(8,128)(2,1)} %param.8) | copy-start | bytes 3145732
  87.1 6.1 %collective-permute-start.10 = (bf16[1,4,128,128]{3,2,1,0:T(8,128)(2,1)S(1)}, bf16[1,4,128,128]{3,2,1,0:T(8,128)(2,1)S(1)}, u32[]{:S(2)}, u32[]{:S(2)}) collective-permute-start(bf16[1,4,128,128]{3,2,1,0:T(8,128)(2,1)S(1)} %get-tuple-element.32), channel_id=1, source_target_pairs={{0,1},{1,2},{2,3},{3,4},{4,5},{5,6},{6,7},{8,9},{9,10},{10,11},{11... | collective-permute-start | bytes 393224 | tf_op jit(solution)/shard_map/ppermute | solution.py:33
  91.2 5.7 %collective-permute-start.11 = (bf16[1,4,128,128]{3,2,1,0:T(8,128)(2,1)S(1)}, bf16[1,4,128,128]{3,2,1,0:T(8,128)(2,1)S(1)}, u32[]{:S(2)}, u32[]{:S(2)}) collective-permute-start(bf16[1,4,128,128]{3,2,1,0:T(8,128)(2,1)S(1)} %get-tuple-element.33), channel_id=1, source_target_pairs={{1,0},{2,1},{3,2},{4,3},{5,4},{6,5},{7,6},{9,8},{10,9},{11,10},{12... | collective-permute-start | bytes 393224 | tf_op jit(solution)/shard_map/ppermute | solution.py:35
  106.0 14.6 %copy-start.5 = (bf16[262144]{0:T(1024)(128)(2,1)}, bf16[262144]{0:T(1024)(128)(2,1)S(1)}, u32[]{:S(2)}) copy-start(bf16[262144]{0:T(1024)(128)(2,1)S(1)} %convert_element_type.469) | copy-start | bytes 1572868
  106.0 12.2 %copy-start.3 = (bf16[262144]{0:T(1024)(128)(2,1)S(1)}, bf16[262144]{0:T(1024)(128)(2,1)}, u32[]{:S(2)}) copy-start(bf16[262144]{0:T(1024)(128)(2,1)} %copy-done.2) | copy-start | bytes 1572868
  106.1 7.6 %collective-permute-start.12 = (bf16[1,4,128,128]{3,2,1,0:T(8,128)(2,1)S(1)}, bf16[1,4,128,128]{3,2,1,0:T(8,128)(2,1)S(1)}, u32[]{:S(2)}, u32[]{:S(2)}) collective-permute-start(bf16[1,4,128,128]{3,2,1,0:T(8,128)(2,1)S(1)} %get-tuple-element.30), channel_id=1, source_target_pairs={{0,1},{1,2},{2,3},{3,4},{4,5},{5,6},{6,7},{8,9},{9,10},{10,11},{11... | collective-permute-start | bytes 393224 | tf_op jit(solution)/shard_map/ppermute | solution.py:33
  111.7 6.4 %collective-permute-start.13 = (bf16[1,4,128,128]{3,2,1,0:T(8,128)(2,1)S(1)}, bf16[1,4,128,128]{3,2,1,0:T(8,128)(2,1)S(1)}, u32[]{:S(2)}, u32[]{:S(2)}) collective-permute-start(bf16[1,4,128,128]{3,2,1,0:T(8,128)(2,1)S(1)} %get-tuple-element.31), channel_id=1, source_target_pairs={{1,0},{2,1},{3,2},{4,3},{5,4},{6,5},{7,6},{9,8},{10,9},{11,10},{12... | collective-permute-start | bytes 393224 | tf_op jit(solution)/shard_map/ppermute | solution.py:35
  127.2 0.8 copy-start.7
  128.0 4.1 %collective-permute-start.14 = (bf16[1,4,128,128]{3,2,1,0:T(8,128)(2,1)S(1)}, bf16[1,4,128,128]{3,2,1,0:T(8,128)(2,1)S(1)}, u32[]{:S(2)}, u32[]{:S(2)}) collective-permute-start(bf16[1,4,128,128]{3,2,1,0:T(8,128)(2,1)S(1)} %get-tuple-element.28), channel_id=1, source_target_pairs={{0,1},{1,2},{2,3},{3,4},{4,5},{5,6},{6,7},{8,9},{9,10},{10,11},{11... | collective-permute-start | bytes 393224 | tf_op jit(solution)/shard_map/ppermute | solution.py:33
  130.2 6.0 %collective-permute-start.15 = (bf16[1,4,128,128]{3,2,1,0:T(8,128)(2,1)S(1)}, bf16[1,4,128,128]{3,2,1,0:T(8,128)(2,1)S(1)}, u32[]{:S(2)}, u32[]{:S(2)}) collective-permute-start(bf16[1,4,128,128]{3,2,1,0:T(8,128)(2,1)S(1)} %get-tuple-element.29), channel_id=1, source_target_pairs={{1,0},{2,1},{3,2},{4,3},{5,4},{6,5},{7,6},{9,8},{10,9},{11,10},{12... | collective-permute-start | bytes 393224 | tf_op jit(solution)/shard_map/ppermute | solution.py:35
  131.5 5.9 %copy-start.8 = (bf16[262144]{0:T(1024)(128)(2,1)S(1)}, bf16[262144]{0:T(1024)(128)(2,1)}, u32[]{:S(2)}) copy-start(bf16[262144]{0:T(1024)(128)(2,1)} %copy-done.7) | copy-start | bytes 1572868
  147.2 1.2 copy-start.4
  147.2 1.4 copy-start.6
  147.2 1.5 copy-start.9
  147.3 3.6 %copy-start.11 = (bf16[262144]{0:T(1024)(128)(2,1)}, bf16[262144]{0:T(1024)(128)(2,1)S(1)}, u32[]{:S(2)}) copy-start(bf16[262144]{0:T(1024)(128)(2,1)S(1)} %convert_element_type.471) | copy-start | bytes 1572868
  151.7 8.1 %collective-permute-start.16 = (f32[1024,128]{1,0:T(8,128)}, f32[1024,128]{1,0:T(8,128)}, u32[]{:S(2)}, u32[]{:S(2)}) collective-permute-start(f32[1024,128]{1,0:T(8,128)} %constant_dynamic-slice_fusion.4), channel_id=1, source_target_pairs={{0,8},{8,0},{1,9},{9,1},{2,10},{10,2},{3,11},{11,3},{4,12},{12,4},... | collective-permute-start | bytes 1572872 | tf_op jit(solution)/shard_map/ppermute | solution.py:140
  160.9 0.8 copy-start.17
  161.7 15.0 %collective-permute-start.17 = (f32[512,128]{1,0:T(8,128)S(1)}, f32[512,128]{1,0:T(8,128)S(1)}, u32[]{:S(2)}, u32[]{:S(2)}) collective-permute-start(f32[512,128]{1,0:T(8,128)S(1)} %constant_dynamic-slice_fusion.3), channel_id=1, source_target_pairs={{0,16},{16,0},{32,48},{48,32},{1,17},{17,1},{33,49},{49,33},{2,18}... | collective-permute-start | bytes 786440 | tf_op jit(solution)/shard_map/ppermute | solution.py:140
  177.7 59.3 %copy-start.10 = (bf16[262144]{0:T(1024)(128)(2,1)S(1)}, bf16[262144]{0:T(1024)(128)(2,1)}, u32[]{:S(2)}) copy-start(bf16[262144]{0:T(1024)(128)(2,1)} %copy-done.7) | copy-start | bytes 1572868
  177.7 59.3 %copy-start.12 = (bf16[262144]{0:T(1024)(128)(2,1)S(1)}, bf16[262144]{0:T(1024)(128)(2,1)}, u32[]{:S(2)}) copy-start(bf16[262144]{0:T(1024)(128)(2,1)} %copy-done.11) | copy-start | bytes 1572868
  177.7 8.8 %collective-permute-start.18 = (f32[256,128]{1,0:T(8,128)S(1)}, f32[256,128]{1,0:T(8,128)}, u32[]{:S(2)}, u32[]{:S(2)}) collective-permute-start(f32[256,128]{1,0:T(8,128)S(1)} %constant_dynamic-slice_fusion.2), channel_id=1, source_target_pairs={{0,32},{16,48},{32,0},{48,16},{1,33},{17,49},{33,1},{49,17},{2,34}... | collective-permute-start | bytes 393224 | tf_op jit(solution)/shard_map/ppermute | solution.py:140
  187.5 3.4 %collective-permute-start.19 = (f32[128,128]{1,0:T(8,128)S(1)}, f32[128,128]{1,0:T(8,128)S(1)}, u32[]{:S(2)}, u32[]{:S(2)}) collective-permute-start(f32[128,128]{1,0:T(8,128)S(1)} %constant_dynamic-slice_fusion.1), channel_id=1, source_target_pairs={{0,64},{64,0},{128,192},{192,128},{1,65},{65,1},{129,193},{193,129... | collective-permute-start | bytes 196616 | tf_op jit(solution)/shard_map/ppermute | solution.py:140
  190.9 4.4 %collective-permute-start.20 = (f32[64,128]{1,0:T(8,128)S(1)}, f32[64,128]{1,0:T(8,128)S(1)}, u32[]{:S(2)}, u32[]{:S(2)}) collective-permute-start(f32[64,128]{1,0:T(8,128)S(1)} %constant_dynamic-slice_fusion), channel_id=1, source_target_pairs={{0,128},{64,192},{128,0},{192,64},{1,129},{65,193},{129,1},{193,65... | collective-permute-start | bytes 98312 | tf_op jit(solution)/shard_map/ppermute | solution.py:140
  195.2 4.4 %collective-permute-start.21 = (f32[64,128]{1,0:T(8,128)S(1)}, f32[64,128]{1,0:T(8,128)S(1)}, u32[]{:S(2)}, u32[]{:S(2)}) collective-permute-start(f32[64,128]{1,0:T(8,128)S(1)} %dynamic-slice_add_fusion.4), channel_id=1, source_target_pairs={{0,128},{64,192},{128,0},{192,64},{1,129},{65,193},{129,1},{193,65... | collective-permute-start | bytes 98312 | tf_op jit(solution)/shard_map/ppermute | solution.py:143
  199.7 3.2 %collective-permute-start.22 = (f32[128,128]{1,0:T(8,128)S(1)}, f32[128,128]{1,0:T(8,128)S(1)}, u32[]{:S(2)}, u32[]{:S(2)}) collective-permute-start(f32[128,128]{1,0:T(8,128)S(1)} %maximum_select_fusion.4), channel_id=1, source_target_pairs={{0,64},{64,0},{128,192},{192,128},{1,65},{65,1},{129,193},{193,129... | collective-permute-start | bytes 196616 | tf_op jit(solution)/shard_map/ppermute | solution.py:143
  202.9 7.9 %collective-permute-start.23 = (f32[256,128]{1,0:T(8,128)S(1)}, f32[256,128]{1,0:T(8,128)}, u32[]{:S(2)}, u32[]{:S(2)}) collective-permute-start(f32[256,128]{1,0:T(8,128)S(1)} %maximum_select_fusion.3), channel_id=1, source_target_pairs={{0,32},{16,48},{32,0},{48,16},{1,33},{17,49},{33,1},{49,17},{2,34}... | collective-permute-start | bytes 393224 | tf_op jit(solution)/shard_map/ppermute | solution.py:143
  211.8 11.9 %collective-permute-start.24 = (f32[512,128]{1,0:T(8,128)S(1)}, f32[512,128]{1,0:T(8,128)}, u32[]{:S(2)}, u32[]{:S(2)}) collective-permute-start(f32[512,128]{1,0:T(8,128)S(1)} %maximum_select_fusion.2), channel_id=1, source_target_pairs={{0,16},{16,0},{32,48},{48,32},{1,17},{17,1},{33,49},{49,33},{2,18}... | collective-permute-start | bytes 786440 | tf_op jit(solution)/shard_map/ppermute | solution.py:143
  225.6 13.2 %collective-permute-start.25 = (f32[1024,128]{1,0:T(8,128)}, f32[1024,128]{1,0:T(8,128)}, u32[]{:S(2)}, u32[]{:S(2)}) collective-permute-start(f32[1024,128]{1,0:T(8,128)} %maximum_select_fusion.1), channel_id=1, source_target_pairs={{0,8},{8,0},{1,9},{9,1},{2,10},{10,2},{3,11},{11,3},{4,12},{12,4},... | collective-permute-start | bytes 1572872 | tf_op jit(solution)/shard_map/ppermute | solution.py:143

commit v2 on v1

--- a/solution.py
+++ b/solution.py
@@ -147,46 +147,96 @@
     return rows.reshape(gradient.shape)
 
 
+def edges(cells, width):
+    count = lax.axis_size(DEPTH)
+    below = lax.ppermute(cells[:, -width:], DEPTH, [(i, i + 1) for i in range(count - 1)])
+    above = lax.ppermute(cells[:, :width], DEPTH, [(i + 1, i) for i in range(count - 1)])
+    return below, above
+
+
+def around(cells, below, above, width):
+    depth = below.shape[1]
+    return jnp.concatenate(
+        [below[:, depth - width :], cells, above[:, :width]], axis=1
+    )
+
+
+def leap(current, earlier, model, stencil, extra):
+    updated = 2.0 * current.astype(jnp.float32) - earlier.astype(jnp.float32) + model * stencil
+    return updated + extra
+
+
 def body(forward_start, adjoint_end, velocity, source_cell, wavelet, receiver_cell, observed):
-    anchor = lax.axis_index(DEPTH) * CZ
-    wave_model = (courant * velocity) ** 2
-    source_ids = source_cell[:, None]
+    depth_len = velocity.shape[0]
+    anchor = lax.axis_index(DEPTH) * depth_len
+    wide = anchor - 4
+    wave_model = ((courant * velocity) ** 2)[None]
+    model_below, model_above = edges(wave_model, 4)
+    model_wide = around(wave_model, model_below, model_above, 4)
+    zeros_own = jnp.zeros(forward_start.shape[1:], jnp.float32)
+    zeros_wide = jnp.zeros(model_wide.shape, jnp.float32)
+
+    def source(moment, zeros, base):
+        return inject_one(zeros, source_cell, wavelet[:, moment : moment + 1], base)
+
+    first, second = forward_start[0], forward_start[1]
+    pair_below, pair_above = edges(
+        jnp.concatenate([first[:, :4], second[:, :8], first[:, -4:], second[:, -8:]], axis=1), 12
+    )
     images = []
     residuals = []
-    earlier = forward_start[0]
-    current = forward_start[1]
-    for moment in range(STEPS):
-        padded = padded_2(current, ((DEPTH, 1),), 4)
-        laplacian = laplace(padded.astype(jnp.float32))
-        updated = (
-            2.0 * current.astype(jnp.float32) - earlier.astype(jnp.float32) + wave_model * laplacian
-        )
-        updated = inject_one(updated, source_cell, wavelet[:, moment : moment + 1], anchor).astype(
-            jnp.bfloat16
-        )
-        images.append(laplacian.astype(jnp.bfloat16))
-        residuals.append(record_rows(updated, receiver_cell, anchor) - observed[:, moment])
-        earlier, current = (current, updated)
+    second_pad = jnp.concatenate([pair_below[:, 4:12], second, pair_above[:, 4:12]], axis=1)
+    first_wide = jnp.concatenate([pair_below[:, 0:4], first, pair_above[:, 0:4]], axis=1)
+    stencil = laplace(second_pad.astype(jnp.float32))
+    wide_next = leap(second_pad[:, 4:-4], first_wide, model_wide, stencil, source(0, zeros_wide, wide)).astype(jnp.bfloat16)
+    images.append(stencil[:, 4:-4].astype(jnp.bfloat16))
+    residuals.append(record_rows(wide_next, receiver_cell, wide) - observed[:, 0])
+    stencil = laplace(wide_next.astype(jnp.float32))
+    own_next = leap(wide_next[:, 4:-4], second, wave_model, stencil, source(1, zeros_own, anchor)).astype(jnp.bfloat16)
+    images.append(stencil.astype(jnp.bfloat16))
+    residuals.append(record_rows(own_next, receiver_cell, anchor) - observed[:, 1])
+    below, above = edges(own_next, 8)
+    third_pad = around(own_next, below, above, 8)
+    stencil = laplace(third_pad.astype(jnp.float32))
+    wide_four = leap(third_pad[:, 4:-4], wide_next, model_wide, stencil, source(2, zeros_wide, wide)).astype(jnp.bfloat16)
+    images.append(stencil[:, 4:-4].astype(jnp.bfloat16))
+    residuals.append(record_rows(wide_four, receiver_cell, wide) - observed[:, 2])
+    stencil = laplace(wide_four.astype(jnp.float32))
+    own_five = leap(wide_four[:, 4:-4], own_next, wave_model, stencil, source(3, zeros_own, anchor)).astype(jnp.bfloat16)
+    images.append(stencil.astype(jnp.bfloat16))
+    residuals.append(record_rows(own_five, receiver_cell, anchor) - observed[:, 3])
+    forward_end = jnp.stack([wide_four[:, 4:-4], own_five])
     images = list(lax.optimization_barrier(tuple(images)))
-    nearer = adjoint_end[0]
-    farther = adjoint_end[1]
+
+    injected = [
+        inject(zeros_own, receiver_cell, residuals[0], anchor),
+        inject(zeros_own, receiver_cell, residuals[1], anchor),
+        inject(zeros_wide, receiver_cell, residuals[2], wide),
+        inject(zeros_own, receiver_cell, residuals[3], anchor),
+    ]
+    nearer, farther = adjoint_end[0], adjoint_end[1]
+    below, above = edges(nearer, 4)
+    five_pad = around(nearer, below, above, 4)
+    stencil = laplace(five_pad.astype(jnp.float32))
+    q4 = leap(nearer, farther, wave_model, stencil, injected[3]).astype(jnp.bfloat16)
+    below, above = edges(q4, 8)
+    four_pad = around(q4, below, above, 8)
+    stencil = laplace(four_pad.astype(jnp.float32))
+    q3_wide = leap(four_pad[:, 4:-4], five_pad, model_wide, stencil, injected[2]).astype(jnp.bfloat16)
+    stencil = laplace(q3_wide.astype(jnp.float32))
+    q2 = leap(q3_wide[:, 4:-4], q4, wave_model, stencil, injected[1]).astype(jnp.bfloat16)
+    below, above = edges(q2, 4)
+    two_pad = around(q2, below, above, 4)
+    stencil = laplace(two_pad.astype(jnp.float32))
+    q1 = leap(q2, q3_wide[:, 4:-4], wave_model, stencil, injected[0]).astype(jnp.bfloat16)
+
     gradient = jnp.zeros(velocity.shape, jnp.float32)
-    for moment in reversed(range(STEPS)):
-        padded = padded_2(nearer, ((DEPTH, 1),), 4)
-        laplacian = laplace(padded.astype(jnp.float32))
-        updated = (
-            2.0 * nearer.astype(jnp.float32) - farther.astype(jnp.float32) + wave_model * laplacian
-        )
-        updated = inject(updated, receiver_cell, residuals[moment], anchor).astype(jnp.bfloat16)
-        gradient = gradient + jnp.sum(
-            updated.astype(jnp.float32) * images[moment].astype(jnp.float32), axis=0
-        )
-        farther, nearer = (nearer, updated)
+    for field, image in ((q4, images[3]), (q3_wide[:, 4:-4], images[2]), (q2, images[1]), (q1, images[0])):
+        gradient = gradient + jnp.sum(field.astype(jnp.float32) * image.astype(jnp.float32), axis=0)
     step_scale = step_base / math.sqrt(forward_start.shape[1] * lax.axis_size(SHOT))
     summed = reduce_shots(gradient)
     velocity_new = jnp.clip(velocity - step_scale * summed, low_speed, high_speed)
-    forward_end = jnp.stack([earlier, current])
-    adjoint_start = jnp.stack([nearer, farther])
+    adjoint_start = jnp.stack([q1, q2])
     return (forward_end, adjoint_start, velocity_new)
 
 

time: 243 us -> 246 us (1.012)
  waiting for transfers between devices: 63.4 us -> 38.7 us
  other arithmetic: 70.6 us -> 93.3 us
  local copies, waits for them, and re-layouts: 22 us -> 36.1 us
  starting transfers between devices: 83.4 us -> 74 us
    convert_element_type x20 -> x13, other arithmetic: 18.9 us -> 44.3 us  [the longest x1 7.75 us: body(): stencil = laplace(wide_four.astype(jnp.float32))]
    ppermute x16 -> x12, waiting for transfers between devices: 25.6 us -> 3.78 us  [the longest x6 3.76 us: edges(): lax.ppermute(cells[:, :width], DEPTH, [(i + 1, i) for i in range(count -...]
    slice x9 -> x14, local copies, waits for them, and re-layouts: 0.82 us -> 11.8 us  [the longest x5 3.18 us: edges(): cells[:, -width:]]
    ppermute x16 -> x12, starting transfers between devices: 42.4 us -> 33.4 us  [the longest x6 25.3 us: edges(): lax.ppermute(cells[:, -width:], DEPTH, [(i, i + 1) for i in range(count -...]
    add x5 -> x1, other arithmetic: 13.5 us -> 4.7 us  [body(): gradient + jnp.sum(field.astype(jnp.float32) * image.astype(jnp.float32),...]
    unnamed x7 -> x10, other arithmetic: 26.2 us -> 30 us
    gather x4, local copies, waits for them, and re-layouts: 16 us -> 19.2 us  [record_rows(): picked = table[row_ids[0]].astype(jnp.float32)]
    ppermute x5, starting transfers between devices: 20 us -> 16.9 us  [reduce_shots(): rows = keep + lax.ppermute(send, axis, perm)]
  transfers between devices with their start and end apart: 26 -> 22, of which waited for: 20 -> 10; matrix products, arithmetic and copies ran while one was open for 11% -> 25% of each run, Pallas kernels for 0% -> 0%
where the time goes in v2:
time: 246 us; the launch traced here: 244 us
  other arithmetic  93.3 us (38%)
  starting transfers between devices  74 us (30%)
  waiting for transfers between devices  38.7 us (16%)
  local copies, waits for them, and re-layouts  36.1 us (15%)
    unnamed x10, other arithmetic  30 us
    ppermute x6, starting transfers between devices, edges(): lax.ppermute(cells[:, -width:], DEPTH, [(i, i + 1) for i in range(count -...  25.3 us
    ppermute x5, starting transfers between devices, reduce_shots(): other = lax.ppermute(rows, axis, perm)  23.7 us
    ppermute x5, waiting for transfers between devices, reduce_shots(): rows = keep + lax.ppermute(send, axis, perm)  19.6 us
    gather x4, local copies, waits for them, and re-layouts, record_rows(): picked = table[row_ids[0]].astype(jnp.float32)  19.2 us
    ppermute x5, starting transfers between devices, reduce_shots(): rows = keep + lax.ppermute(send, axis, perm)  16.9 us
    ppermute x5, waiting for transfers between devices, reduce_shots(): other = lax.ppermute(rows, axis, perm)  15.3 us
    ppermute x6, starting transfers between devices, edges(): lax.ppermute(cells[:, :width], DEPTH, [(i + 1, i) for i in range(count -...  8.03 us
  transfers between devices with their start and end apart: 22, of which 10 were waited for; matrix products, arithmetic and copies ran while one was open for 25% of the time, Pallas kernels for 0%

profile of v2, /device:TPU:1, one launch (start us, length us, event | category | flops | bytes accessed | tf_op | source)
XLA Modules:
  0.0 244.0 jit_solution(16216646204789963998)
XLA Ops:
  0.6 1.3 slice_bitcast_fusion.2
  2.8 5.1 %collective-permute-start = (bf16[1,12,128,128]{3,2,1,0:T(8,128)(2,1)}, bf16[1,12,128,128]{3,2,1,0:T(8,128)(2,1)}, u32[]{:S(2)}, u32[]{:S(2)}) collective-permute-start(bf16[1,12,128,128]{3,2,1,0:T(8,128)(2,1)} %pad_maximum_fusion.6), channel_id=1, source_target_pairs={{0,1},{1,2},{2,3},{3,4},{4,5},{5,6},{6,7},{8,9},{9,10},{10,11},{11... | collective-permute-start | bytes 1179656 | tf_op jit(solution)/shard_map/ppermute | solution.py:152
  8.7 1.4 collective-permute-start.1
  11.1 4.0 %collective-permute-start.2 = (f32[1,4,128,128]{3,2,1,0:T(8,128)}, f32[1,4,128,128]{3,2,1,0:T(8,128)S(1)}, u32[]{:S(2)}, u32[]{:S(2)}) collective-permute-start(f32[1,4,128,128]{3,2,1,0:T(8,128)} %get-tuple-element.43), channel_id=1, source_target_pairs={{0,1},{1,2},{2,3},{3,4},{4,5},{5,6},{6,7},{8,9},{9,10},{10,11},{11... | collective-permute-start | bytes 786440 | tf_op jit(solution)/shard_map/ppermute | solution.py:152
  15.1 1.3 collective-permute-start.3
  18.0 4.0 %collective-permute-start.6 = (bf16[1,4,128,128]{3,2,1,0:T(8,128)(2,1)}, bf16[1,4,128,128]{3,2,1,0:T(8,128)(2,1)S(1)}, u32[]{:S(2)}, u32[]{:S(2)}) collective-permute-start(bf16[1,4,128,128]{3,2,1,0:T(8,128)(2,1)} %get-tuple-element.49), channel_id=1, source_target_pairs={{0,1},{1,2},{2,3},{3,4},{4,5},{5,6},{6,7},{8,9},{9,10},{10,11},{11... | collective-permute-start | bytes 393224 | tf_op jit(solution)/shard_map/ppermute | solution.py:152
  25.0 1.3 collective-permute-start.7
  27.2 1.6 slice.1048
  29.8 1.6 slice.1049
  31.4 1.2 fusion.233
  32.5 3.7 %collective-permute-done.3 = f32[1,4,128,128]{3,2,1,0:T(8,128)S(1)} collective-permute-done((f32[1,4,128,128]{3,2,1,0:T(8,128)}, f32[1,4,128,128]{3,2,1,0:T(8,128)S(1)}, u32[]{:S(2)}, u32[]{:S(2)}) %collective-permute-start.3) | collective-permute-done | bytes 262176 | tf_op jit(solution)/shard_map/ppermute | solution.py:153
  37.0 7.7 %fusion.243 = (f32[1,24,128,128]{3,2,1,0:T(8,128)S(1)}, bf16[1,24,128,128]{3,2,1,0:T(8,128)(2,1)S(1)}, bf16[1,24,128,128]{3,2,1,0:T(8,128)(2,1)}) fusion(f32[]{:T(128)} %bitcast.7, s32[]{:T(128)} %bitcast.6, s32[]{:T(128)} %bitcast.5, s32[]{:T(128)} %bitcast.4, f32[1,4,128,128]{3,2,1,0:T(8,128)} %copy-done.21, ...), kind=kLoop, calls=%fused_computation.500 | loop fusion | flops 20447232 | bytes 22544400 | tf_op jit(solution)/shard_map/convert_element_type | solution.py:194
  44.7 3.1 %fusion.237 = (bf16[1,16,128,128]{3,2,1,0:T(8,128)(2,1)}, f32[1,16,128,128]{3,2,1,0:T(8,128)S(1)}) fusion(f32[1,24,128,128]{3,2,1,0:T(8,128)S(1)} %get-tuple-element.32), kind=kLoop, calls=%fused_computation.497 | loop fusion | flops 7864320 | bytes 12582912 | tf_op jit(solution)/shard_map/convert_element_type | solution.py:196
  47.8 1.2 add_convert_fusion.3
  49.8 4.3 %collective-permute-start.4 = (bf16[1,8,128,128]{3,2,1,0:T(8,128)(2,1)}, bf16[1,8,128,128]{3,2,1,0:T(8,128)(2,1)}, u32[]{:S(2)}, u32[]{:S(2)}) collective-permute-start(bf16[1,8,128,128]{3,2,1,0:T(8,128)(2,1)} %get-tuple-element.51), channel_id=1, source_target_pairs={{0,1},{1,2},{2,3},{3,4},{4,5},{5,6},{6,7},{8,9},{9,10},{10,11},{11... | collective-permute-start | bytes 786440 | tf_op jit(solution)/shard_map/ppermute | solution.py:152
  54.1 1.5 collective-permute-start.5
  57.3 4.3 %gather_fusion.2 = bf16[1024,128]{1,0:T(8,128)(2,1)} fusion(bf16[2048,128]{1,0:T(8,128)(2,1)S(1)} %bitcast.86, s32[1024]{0:T(1024)S(1)} %broadcast_clamp_fusion.1), kind=kCustom, calls=%fused_computation.2 | custom fusion | bytes 528384 | tf_op jit(solution)/shard_map/gather | solution.py:109
  61.6 5.3 %gather_fusion.3 = bf16[1024,128]{1,0:T(8,128)(2,1)} fusion(bf16[3072,128]{1,0:T(8,128)(2,1)} %bitcast.87, s32[1024]{0:T(1024)S(1)} %broadcast_clamp_fusion), kind=kCustom, calls=%fused_computation.3 | custom fusion | bytes 528384 | tf_op jit(solution)/shard_map/gather | solution.py:109
  66.9 2.3 fusion.232
  69.2 7.7 %fusion.241 = (f32[1,24,128,128]{3,2,1,0:T(8,128)S(1)}, bf16[1,24,128,128]{3,2,1,0:T(8,128)(2,1)}, bf16[1,24,128,128]{3,2,1,0:T(8,128)(2,1)}) fusion(f32[]{:T(128)} %bitcast.11, s32[]{:T(128)} %bitcast.6, s32[]{:T(128)} %bitcast.5, s32[]{:T(128)} %bitcast.4, f32[1,4,128,128]{3,2,1,0:T(8,128)S(1)} %copy-done.22, f32[1,16,128,128]{3,2,1,0:T(8,128)} %copy-done.3, ...), kind=kLoop, calls=%fused_computation.499 | loop fusion | flops 18481152 | bytes 22544400 | tf_op jit(solution)/shard_map/convert_element_type | solution.py:204
  77.0 3.1 %fusion.235 = (bf16[1,16,128,128]{3,2,1,0:T(8,128)(2,1)}, f32[1,16,128,128]{3,2,1,0:T(8,128)S(1)}) fusion(f32[1,24,128,128]{3,2,1,0:T(8,128)S(1)} %get-tuple-element.29), kind=kLoop, calls=%fused_computation.496 | loop fusion | flops 7864320 | bytes 12582912 | tf_op jit(solution)/shard_map/convert_element_type | solution.py:206
  80.1 1.8 add_convert_fusion.2
  81.8 5.3 %gather_fusion = bf16[1024,128]{1,0:T(8,128)(2,1)} fusion(bf16[2048,128]{1,0:T(8,128)(2,1)} %bitcast.89, s32[1024]{0:T(1024)S(1)} %broadcast_clamp_fusion.1), kind=kCustom, calls=%fused_computation | custom fusion | bytes 528384 | tf_op jit(solution)/shard_map/gather | solution.py:109
  87.1 4.3 %gather_fusion.1 = bf16[1024,128]{1,0:T(8,128)(2,1)} fusion(bf16[3072,128]{1,0:T(8,128)(2,1)S(1)} %bitcast.88, s32[1024]{0:T(1024)S(1)} %broadcast_clamp_fusion), kind=kCustom, calls=%fused_computation.1 | custom fusion | bytes 528384 | tf_op jit(solution)/shard_map/gather | solution.py:109
  91.4 1.8 select_reduce_fusion
  93.2 1.5 fusion.228
  94.7 7.0 %scatter_custom_fusion = f32[262144]{0:T(1024)} fusion(s32[1024]{0:T(1024)} %broadcast_select_fusion.1, f32[1024]{0:T(1024)S(1)} %bitcast.110, f32[]{:T(128)} %constant.308.clone.1), kind=kCustom, calls=%fused_computation.430 | custom fusion | flops 1024 | bytes 1049088
  101.8 3.7 %fusion.215 = bf16[1,16,128,128]{3,2,1,0:T(8,128)(2,1)S(1)} fusion(f32[1,16,128,128]{3,2,1,0:T(8,128)} %bitcast.94, f32[1,24,128,128]{3,2,1,0:T(8,128)S(1)} %maximum_convert_fusion, bf16[2,1,16,128,128]{4,3,2,1,0:T(8,128)(2,1)} %param.8, f32[16,128,128]{2,1,0:T(8,128)S(1)} %copy-done), kind=kLoop, calls=%fused_computation.420 | loop fusion | flops 10223616 | bytes 14680064 | tf_op jit(solution)/shard_map/convert_element_type | solution.py:221
  105.5 4.0 %collective-permute-start.8 = (bf16[1,8,128,128]{3,2,1,0:T(8,128)(2,1)S(1)}, bf16[1,8,128,128]{3,2,1,0:T(8,128)(2,1)S(1)}, u32[]{:S(2)}, u32[]{:S(2)}) collective-permute-start(bf16[1,8,128,128]{3,2,1,0:T(8,128)(2,1)S(1)} %get-tuple-element.47), channel_id=1, source_target_pairs={{0,1},{1,2},{2,3},{3,4},{4,5},{5,6},{6,7},{8,9},{9,10},{10,11},{11... | collective-permute-start | bytes 786440 | tf_op jit(solution)/shard_map/ppermute | solution.py:152
  109.5 1.3 collective-permute-start.9
  110.9 7.0 %scatter_custom_fusion.2 = f32[262144]{0:T(1024)} fusion(s32[1024]{0:T(1024)} %broadcast_select_fusion.1, f32[1024]{0:T(1024)S(1)} %bitcast.109, f32[]{:T(128)} %constant.308.clone.1), kind=kCustom, calls=%fused_computation.428 | custom fusion | flops 1024 | bytes 1049088
  118.0 7.2 %scatter_custom_fusion.1 = f32[393216]{0:T(1024)} fusion(s32[1024]{0:T(1024)S(1)} %broadcast_select_fusion, f32[1024]{0:T(1024)S(1)} %bitcast.108, f32[]{:T(128)} %constant.308.clone.1), kind=kCustom, calls=%fused_computation.423 | custom fusion | flops 1024 | bytes 1572868
  125.1 1.2 pad_maximum_fusion.4
  126.3 6.8 %fusion.239 = (f32[1,24,128,128]{3,2,1,0:T(8,128)S(1)}, bf16[1,24,128,128]{3,2,1,0:T(8,128)(2,1)}) fusion(f32[1,24,128,128]{3,2,1,0:T(8,128)} %bitcast.92, f32[1,32,128,128]{3,2,1,0:T(8,128)S(1)} %get-tuple-element.36, f32[1,4,128,128]{3,2,1,0:T(8,128)} %copy-done.21, f32[1,16,128,128]{3,2,1,0:T(8,128)} %copy-done.3, f32[1,4,128,128]{3,2,1,0:T(8,128)S(1)} %copy-done.20, ...), kind=kLoop, calls=%fused_computation.498 | loop fusion | flops 16515072 | bytes 23330816 | tf_op jit(solution)/shard_map/convert_element_type | solution.py:226
  133.1 3.7 %fusion.80 = bf16[1,16,128,128]{3,2,1,0:T(8,128)(2,1)S(1)} fusion(f32[1,16,128,128]{3,2,1,0:T(8,128)} %bitcast.93, bf16[1,16,128,128]{3,2,1,0:T(8,128)(2,1)} %copy-done.8, f32[1,24,128,128]{3,2,1,0:T(8,128)S(1)} %get-tuple-element.21, bf16[1,24,128,128]{3,2,1,0:T(8,128)(2,1)} %get-tuple-element.22, f32[16,128,128]{2,1,0:T(8,128)S(1)} %copy-done), kind=kLoop, calls=%fused_computation.244 | loop fusion | flops 10223616 | bytes 14680064 | tf_op jit(solution)/shard_map/convert_element_type | solution.py:227
  138.3 4.0 %collective-permute-start.10 = (bf16[1,4,128,128]{3,2,1,0:T(8,128)(2,1)}, bf16[1,4,128,128]{3,2,1,0:T(8,128)(2,1)S(1)}, u32[]{:S(2)}, u32[]{:S(2)}) collective-permute-start(bf16[1,4,128,128]{3,2,1,0:T(8,128)(2,1)} %get-tuple-element.45), channel_id=1, source_target_pairs={{0,1},{1,2},{2,3},{3,4},{4,5},{5,6},{6,7},{8,9},{9,10},{10,11},{11... | collective-permute-start | bytes 393224 | tf_op jit(solution)/shard_map/ppermute | solution.py:152
  142.3 1.3 collective-permute-start.11
  143.6 1.9 slice.2187
  146.4 7.2 %scatter_custom_fusion.3 = f32[262144]{0:T(1024)} fusion(s32[1024]{0:T(1024)} %broadcast_select_fusion.1, f32[1024]{0:T(1024)} %bitcast.107, f32[]{:T(128)} %constant.308.clone.1), kind=kCustom, calls=%fused_computation.426 | custom fusion | flops 1024 | bytes 1049088
  153.6 1.1 maximum_convert_fusion.1
  155.0 4.7 %fusion.83 = (f32[1,16,128,128]{3,2,1,0:T(8,128)S(1)}, bf16[1,16,128,128]{3,2,1,0:T(8,128)(2,1)}) fusion(bf16[1,16,128,128]{3,2,1,0:T(8,128)(2,1)S(1)} %copy-done.9, bf16[1,16,128,128]{3,2,1,0:T(8,128)(2,1)S(1)} %copy-done.11, bf16[1,16,128,128]{3,2,1,0:T(8,128)(2,1)} %slice.2187, bf16[1,16,128,128]{3,2,1,0:T(8,128)(2,1)S(1)} %copy-done.26, ...), kind=kLoop, calls=%fused_computation.247 | loop fusion | flops 13631488 | bytes 18350080 | tf_op jit(solution)/shard_map/add | solution.py:235
  160.7 4.1 %collective-permute-start.12 = (f32[1024,128]{1,0:T(8,128)S(1)}, f32[1024,128]{1,0:T(8,128)S(1)}, u32[]{:S(2)}, u32[]{:S(2)}) collective-permute-start(f32[1024,128]{1,0:T(8,128)S(1)} %constant_dynamic-slice_fusion.4), channel_id=1, source_target_pairs={{0,8},{8,0},{1,9},{9,1},{2,10},{10,2},{3,11},{11,3},{4,12},{12,4},... | collective-permute-start | bytes 1572872 | tf_op jit(solution)/shard_map/ppermute | solution.py:140
  164.9 1.5 collective-permute-done.12
  167.6 3.1 %collective-permute-start.13 = (f32[512,128]{1,0:T(8,128)S(1)}, f32[512,128]{1,0:T(8,128)S(1)}, u32[]{:S(2)}, u32[]{:S(2)}) collective-permute-start(f32[512,128]{1,0:T(8,128)S(1)} %constant_dynamic-slice_fusion.3), channel_id=1, source_target_pairs={{0,16},{16,0},{32,48},{48,32},{1,17},{17,1},{33,49},{49,33},{2,18}... | collective-permute-start | bytes 786440 | tf_op jit(solution)/shard_map/ppermute | solution.py:140
  170.6 11.9 %collective-permute-done.13 = f32[512,128]{1,0:T(8,128)S(1)} collective-permute-done((f32[512,128]{1,0:T(8,128)S(1)}, f32[512,128]{1,0:T(8,128)S(1)}, u32[]{:S(2)}, u32[]{:S(2)}) %collective-permute-start.13) | collective-permute-done | bytes 262176 | tf_op jit(solution)/shard_map/ppermute | solution.py:140
  182.6 5.3 %collective-permute-start.14 = (f32[256,128]{1,0:T(8,128)S(1)}, f32[256,128]{1,0:T(8,128)S(1)}, u32[]{:S(2)}, u32[]{:S(2)}) collective-permute-start(f32[256,128]{1,0:T(8,128)S(1)} %constant_dynamic-slice_fusion.2), channel_id=1, source_target_pairs={{0,32},{16,48},{32,0},{48,16},{1,33},{17,49},{33,1},{49,17},{2,34}... | collective-permute-start | bytes 393224 | tf_op jit(solution)/shard_map/ppermute | solution.py:140
  187.9 2.6 %collective-permute-done.14 = f32[256,128]{1,0:T(8,128)S(1)} collective-permute-done((f32[256,128]{1,0:T(8,128)S(1)}, f32[256,128]{1,0:T(8,128)S(1)}, u32[]{:S(2)}, u32[]{:S(2)}) %collective-permute-start.14) | collective-permute-done | bytes 131104 | tf_op jit(solution)/shard_map/ppermute | solution.py:140
  190.6 1.4 collective-permute-start.15
  192.0 2.1 collective-permute-done.15
  194.1 3.0 %collective-permute-start.16 = (f32[64,128]{1,0:T(8,128)S(1)}, f32[64,128]{1,0:T(8,128)S(1)}, u32[]{:S(2)}, u32[]{:S(2)}) collective-permute-start(f32[64,128]{1,0:T(8,128)S(1)} %constant_dynamic-slice_fusion), channel_id=1, source_target_pairs={{0,128},{64,192},{128,0},{192,64},{1,129},{65,193},{129,1},{193,65... | collective-permute-start | bytes 98312 | tf_op jit(solution)/shard_map/ppermute | solution.py:140
  197.1 1.4 collective-permute-done.16
  198.5 3.3 %collective-permute-start.17 = (f32[64,128]{1,0:T(8,128)S(1)}, f32[64,128]{1,0:T(8,128)S(1)}, u32[]{:S(2)}, u32[]{:S(2)}) collective-permute-start(f32[64,128]{1,0:T(8,128)S(1)} %dynamic-slice_add_fusion.4), channel_id=1, source_target_pairs={{0,128},{64,192},{128,0},{192,64},{1,129},{65,193},{129,1},{193,65... | collective-permute-start | bytes 98312 | tf_op jit(solution)/shard_map/ppermute | solution.py:143
  201.8 1.3 collective-permute-done.17
  203.1 1.1 collective-permute-start.18
  204.2 2.1 collective-permute-done.18
  206.3 5.5 %collective-permute-start.19 = (f32[256,128]{1,0:T(8,128)S(1)}, f32[256,128]{1,0:T(8,128)S(1)}, u32[]{:S(2)}, u32[]{:S(2)}) collective-permute-start(f32[256,128]{1,0:T(8,128)S(1)} %maximum_select_fusion.3), channel_id=1, source_target_pairs={{0,32},{16,48},{32,0},{48,16},{1,33},{17,49},{33,1},{49,17},{2,34}... | collective-permute-start | bytes 393224 | tf_op jit(solution)/shard_map/ppermute | solution.py:143
  211.8 2.4 collective-permute-done.19
  214.2 3.6 %collective-permute-start.20 = (f32[512,128]{1,0:T(8,128)S(1)}, f32[512,128]{1,0:T(8,128)}, u32[]{:S(2)}, u32[]{:S(2)}) collective-permute-start(f32[512,128]{1,0:T(8,128)S(1)} %maximum_select_fusion.2), channel_id=1, source_target_pairs={{0,16},{16,0},{32,48},{48,32},{1,17},{17,1},{33,49},{49,33},{2,18}... | collective-permute-start | bytes 786440 | tf_op jit(solution)/shard_map/ppermute | solution.py:143
  217.9 9.5 %collective-permute-done.20 = f32[512,128]{1,0:T(8,128)} collective-permute-done((f32[512,128]{1,0:T(8,128)S(1)}, f32[512,128]{1,0:T(8,128)}, u32[]{:S(2)}, u32[]{:S(2)}) %collective-permute-start.20) | collective-permute-done | bytes 262176 | tf_op jit(solution)/shard_map/ppermute | solution.py:143
  227.3 1.3 maximum_select_fusion.1
  228.6 10.3 %collective-permute-start.21 = (f32[1024,128]{1,0:T(8,128)S(1)}, f32[1024,128]{1,0:T(8,128)}, u32[]{:S(2)}, u32[]{:S(2)}) collective-permute-start(f32[1024,128]{1,0:T(8,128)S(1)} %maximum_select_fusion.1), channel_id=1, source_target_pairs={{0,8},{8,0},{1,9},{9,1},{2,10},{10,2},{3,11},{11,3},{4,12},{12,4},... | collective-permute-start | bytes 1572872 | tf_op jit(solution)/shard_map/ppermute | solution.py:143
  238.9 2.6 %pad_maximum_fusion.3 = (bf16[2,1,16,128,128]{4,3,2,1,0:T(8,128)(2,1)}, bf16[2,1,16,128,128]{4,3,2,1,0:T(8,128)(2,1)}) fusion(bf16[1,1,16,128,128]{4,3,2,1,0:T(8,128)(2,1)S(1)} %bitcast.90, bf16[1,1,16,128,128]{4,3,2,1,0:T(8,128)(2,1)S(1)} %slice_bitcast_fusion.3, bf16[1,1,16,128,128]{4,3,2,1,0:T(8,128)(2,1)S(1)} %bitcast.91, ...), kind=kLoop, calls=%fused_computation.405 | loop fusion | flops 1048576 | bytes 4194304 | tf_op jit(solution)/shard_map/stack | solution.py:208
  241.5 1.3 fusion.212
  242.8 1.1 subtract_clamp_fusion
  (129 shorter events, 16.7 us)
Async XLA Ops:
  1.9 6.8 %copy-start.17 = (bf16[1,16,128,128]{3,2,1,0:T(8,128)(2,1)}, bf16[1,16,128,128]{3,2,1,0:T(8,128)(2,1)S(1)}, u32[]{:S(2)}) copy-start(bf16[1,16,128,128]{3,2,1,0:T(8,128)(2,1)S(1)} %get-tuple-element.41) | copy-start | bytes 1572868
  1.9 8.2 %copy-start = (f32[16,128,128]{2,1,0:T(8,128)S(1)}, f32[16,128,128]{2,1,0:T(8,128)}, u32[]{:S(2)}) copy-start(f32[16,128,128]{2,1,0:T(8,128)} %param.9) | copy-start | bytes 3145732
  2.8 22.2 %collective-permute-start = (bf16[1,12,128,128]{3,2,1,0:T(8,128)(2,1)}, bf16[1,12,128,128]{3,2,1,0:T(8,128)(2,1)}, u32[]{:S(2)}, u32[]{:S(2)}) collective-permute-start(bf16[1,12,128,128]{3,2,1,0:T(8,128)(2,1)} %pad_maximum_fusion.6), channel_id=1, source_target_pairs={{0,1},{1,2},{2,3},{3,4},{4,5},{5,6},{6,7},{8,9},{9,10},{10,11},{11... | collective-permute-start | bytes 1179656 | tf_op jit(solution)/shard_map/ppermute | solution.py:152
  8.7 7.7 %copy-start.23 = (bf16[2,1,16,128,128]{4,3,2,1,0:T(8,128)(2,1)S(1)}, bf16[2,1,16,128,128]{4,3,2,1,0:T(8,128)(2,1)}, u32[]{:S(2)}) copy-start(bf16[2,1,16,128,128]{4,3,2,1,0:T(8,128)(2,1)} %param.8) | copy-start | bytes 3145732
  8.7 20.1 %collective-permute-start.1 = (bf16[1,12,128,128]{3,2,1,0:T(8,128)(2,1)}, bf16[1,12,128,128]{3,2,1,0:T(8,128)(2,1)}, u32[]{:S(2)}, u32[]{:S(2)}) collective-permute-start(bf16[1,12,128,128]{3,2,1,0:T(8,128)(2,1)} %pad_maximum_fusion.7), channel_id=1, source_target_pairs={{1,0},{2,1},{3,2},{4,3},{5,4},{6,5},{7,6},{9,8},{10,9},{11,10},{12... | collective-permute-start | bytes 1179656 | tf_op jit(solution)/shard_map/ppermute | solution.py:153
  10.2 26.8 %copy-start.3 = (f32[1,16,128,128]{3,2,1,0:T(8,128)}, f32[1,16,128,128]{3,2,1,0:T(8,128)S(1)}, u32[]{:S(2)}) copy-start(f32[1,16,128,128]{3,2,1,0:T(8,128)S(1)} %multiply_bitcast_fusion) | copy-start | bytes 3145732
  10.2 11.8 %copy-start.32 = (s32[1,1024]{1,0:T(1,128)S(1)}, s32[1,1024]{1,0:T(1,128)}, u32[]{:S(2)}) copy-start(s32[1,1024]{1,0:T(1,128)} %param.12) | copy-start | bytes 12292
  10.2 12.6 %copy-start.34 = (s32[2]{0:T(128)S(1)}, s32[2]{0:T(128)}, u32[]{:S(2)}) copy-start(s32[2]{0:T(128)} %constant.378) | copy-start | bytes 28
  10.3 12.6 %copy-start.36 = (s32[2]{0:T(128)S(1)}, s32[2]{0:T(128)}, u32[]{:S(2)}) copy-start(s32[2]{0:T(128)} %constant.381) | copy-start | bytes 28
  10.3 14.0 %copy-start.31 = (f32[1,4]{1,0:T(1,128)S(1)}, f32[1,4]{1,0:T(1,128)}, u32[]{:S(2)}) copy-start(f32[1,4]{1,0:T(1,128)} %param.11) | copy-start | bytes 52
  11.1 21.4 %collective-permute-start.2 = (f32[1,4,128,128]{3,2,1,0:T(8,128)}, f32[1,4,128,128]{3,2,1,0:T(8,128)S(1)}, u32[]{:S(2)}, u32[]{:S(2)}) collective-permute-start(f32[1,4,128,128]{3,2,1,0:T(8,128)} %get-tuple-element.43), channel_id=1, source_target_pairs={{0,1},{1,2},{2,3},{3,4},{4,5},{5,6},{6,7},{8,9},{9,10},{10,11},{11... | collective-permute-start | bytes 786440 | tf_op jit(solution)/shard_map/ppermute | solution.py:152
  15.1 21.1 %collective-permute-start.3 = (f32[1,4,128,128]{3,2,1,0:T(8,128)}, f32[1,4,128,128]{3,2,1,0:T(8,128)S(1)}, u32[]{:S(2)}, u32[]{:S(2)}) collective-permute-start(f32[1,4,128,128]{3,2,1,0:T(8,128)} %get-tuple-element.44), channel_id=1, source_target_pairs={{1,0},{2,1},{3,2},{4,3},{5,4},{6,5},{7,6},{9,8},{10,9},{11,10},{12... | collective-permute-start | bytes 786440 | tf_op jit(solution)/shard_map/ppermute | solution.py:153
  16.5 0.8 copy-start.12
  18.0 38.2 %collective-permute-start.6 = (bf16[1,4,128,128]{3,2,1,0:T(8,128)(2,1)}, bf16[1,4,128,128]{3,2,1,0:T(8,128)(2,1)S(1)}, u32[]{:S(2)}, u32[]{:S(2)}) collective-permute-start(bf16[1,4,128,128]{3,2,1,0:T(8,128)(2,1)} %get-tuple-element.49), channel_id=1, source_target_pairs={{0,1},{1,2},{2,3},{3,4},{4,5},{5,6},{6,7},{8,9},{9,10},{10,11},{11... | collective-permute-start | bytes 393224 | tf_op jit(solution)/shard_map/ppermute | solution.py:152
  25.0 31.2 %collective-permute-start.7 = (bf16[1,4,128,128]{3,2,1,0:T(8,128)(2,1)}, bf16[1,4,128,128]{3,2,1,0:T(8,128)(2,1)}, u32[]{:S(2)}, u32[]{:S(2)}) collective-permute-start(bf16[1,4,128,128]{3,2,1,0:T(8,128)(2,1)} %get-tuple-element.50), channel_id=1, source_target_pairs={{1,0},{2,1},{3,2},{4,3},{5,4},{6,5},{7,6},{9,8},{10,9},{11,10},{12... | collective-permute-start | bytes 393224 | tf_op jit(solution)/shard_map/ppermute | solution.py:153
  32.5 3.8 %copy-start.18 = (f32[1,4,128,128]{3,2,1,0:T(8,128)}, f32[1,4,128,128]{3,2,1,0:T(8,128)S(1)}, u32[]{:S(2)}) copy-start(f32[1,4,128,128]{3,2,1,0:T(8,128)S(1)} %collective-permute-done.2) | copy-start | bytes 786436
  36.3 0.7 copy-start.21
  44.7 3.1 %copy-start.1 = (bf16[1,24,128,128]{3,2,1,0:T(8,128)(2,1)}, bf16[1,24,128,128]{3,2,1,0:T(8,128)(2,1)S(1)}, u32[]{:S(2)}) copy-start(bf16[1,24,128,128]{3,2,1,0:T(8,128)(2,1)S(1)} %get-tuple-element.33) | copy-start | bytes 2359300
  44.7 3.1 %copy-start.24 = (bf16[2,1,16,128,128]{4,3,2,1,0:T(8,128)(2,1)S(1)}, bf16[2,1,16,128,128]{4,3,2,1,0:T(8,128)(2,1)}, u32[]{:S(2)}) copy-start(bf16[2,1,16,128,128]{4,3,2,1,0:T(8,128)(2,1)} %param.7) | copy-start | bytes 3145732
  47.8 7.8 %copy-start.33 = (s32[2]{0:T(128)S(1)}, s32[2]{0:T(128)}, u32[]{:S(2)}) copy-start(s32[2]{0:T(128)} %constant.384) | copy-start | bytes 28
  47.8 8.4 %copy-start.13 = (bf16[1,16,128,128]{3,2,1,0:T(8,128)(2,1)S(1)}, bf16[1,16,128,128]{3,2,1,0:T(8,128)(2,1)}, u32[]{:S(2)}) copy-start(bf16[1,16,128,128]{3,2,1,0:T(8,128)(2,1)} %copy-done.12) | copy-start | bytes 1572868
  49.8 17.1 %collective-permute-start.4 = (bf16[1,8,128,128]{3,2,1,0:T(8,128)(2,1)}, bf16[1,8,128,128]{3,2,1,0:T(8,128)(2,1)}, u32[]{:S(2)}, u32[]{:S(2)}) collective-permute-start(bf16[1,8,128,128]{3,2,1,0:T(8,128)(2,1)} %get-tuple-element.51), channel_id=1, source_target_pairs={{0,1},{1,2},{2,3},{3,4},{4,5},{5,6},{6,7},{8,9},{9,10},{10,11},{11... | collective-permute-start | bytes 786440 | tf_op jit(solution)/shard_map/ppermute | solution.py:152
  54.1 12.8 %collective-permute-start.5 = (bf16[1,8,128,128]{3,2,1,0:T(8,128)(2,1)}, bf16[1,8,128,128]{3,2,1,0:T(8,128)(2,1)}, u32[]{:S(2)}, u32[]{:S(2)}) collective-permute-start(bf16[1,8,128,128]{3,2,1,0:T(8,128)(2,1)} %get-tuple-element.52), channel_id=1, source_target_pairs={{1,0},{2,1},{3,2},{4,3},{5,4},{6,5},{7,6},{9,8},{10,9},{11,10},{12... | collective-permute-start | bytes 786440 | tf_op jit(solution)/shard_map/ppermute | solution.py:153
  66.9 2.3 copy-start.2
  66.9 2.3 copy-start.19
  66.9 2.3 copy-start.22
  77.0 3.1 %copy-start.4 = (bf16[1,24,128,128]{3,2,1,0:T(8,128)(2,1)S(1)}, bf16[1,24,128,128]{3,2,1,0:T(8,128)(2,1)}, u32[]{:S(2)}) copy-start(bf16[1,24,128,128]{3,2,1,0:T(8,128)(2,1)} %get-tuple-element.30) | copy-start | bytes 2359300
  81.8 5.3 %copy-start.5 = (bf16[1,24,128,128]{3,2,1,0:T(8,128)(2,1)S(1)}, bf16[1,24,128,128]{3,2,1,0:T(8,128)(2,1)}, u32[]{:S(2)}) copy-start(bf16[1,24,128,128]{3,2,1,0:T(8,128)(2,1)} %get-tuple-element.30) | copy-start | bytes 2359300
  87.1 4.3 %copy-start.29 = (s32[1,1024]{1,0:T(1,128)S(1)}, s32[1,1024]{1,0:T(1,128)}, u32[]{:S(2)}) copy-start(s32[1,1024]{1,0:T(1,128)} %and_select_fusion.2) | copy-start | bytes 12292
  101.8 9.0 %copy-start.35 = (s32[2]{0:T(128)S(1)}, s32[2]{0:T(128)}, u32[]{:S(2)}) copy-start(s32[2]{0:T(128)} %constant.387) | copy-start | bytes 28
  101.8 9.1 %copy-start.30 = (s32[1024]{0:T(1024)S(1)}, s32[1024]{0:T(1024)}, u32[]{:S(2)}) copy-start(s32[1024]{0:T(1024)} %fusion.225) | copy-start | bytes 12292
  105.4 19.7 %copy-start.8 = (bf16[1,16,128,128]{3,2,1,0:T(8,128)(2,1)}, bf16[1,16,128,128]{3,2,1,0:T(8,128)(2,1)S(1)}, u32[]{:S(2)}) copy-start(bf16[1,16,128,128]{3,2,1,0:T(8,128)(2,1)S(1)} %fusion.215) | copy-start | bytes 1572868
  105.5 19.6 %collective-permute-start.8 = (bf16[1,8,128,128]{3,2,1,0:T(8,128)(2,1)S(1)}, bf16[1,8,128,128]{3,2,1,0:T(8,128)(2,1)S(1)}, u32[]{:S(2)}, u32[]{:S(2)}) collective-permute-start(bf16[1,8,128,128]{3,2,1,0:T(8,128)(2,1)S(1)} %get-tuple-element.47), channel_id=1, source_target_pairs={{0,1},{1,2},{2,3},{3,4},{4,5},{5,6},{6,7},{8,9},{9,10},{10,11},{11... | collective-permute-start | bytes 786440 | tf_op jit(solution)/shard_map/ppermute | solution.py:152
  109.5 15.6 %collective-permute-start.9 = (bf16[1,8,128,128]{3,2,1,0:T(8,128)(2,1)S(1)}, bf16[1,8,128,128]{3,2,1,0:T(8,128)(2,1)S(1)}, u32[]{:S(2)}, u32[]{:S(2)}) collective-permute-start(bf16[1,8,128,128]{3,2,1,0:T(8,128)(2,1)S(1)} %get-tuple-element.48), channel_id=1, source_target_pairs={{1,0},{2,1},{3,2},{4,3},{5,4},{6,5},{7,6},{9,8},{10,9},{11,10},{12... | collective-permute-start | bytes 786440 | tf_op jit(solution)/shard_map/ppermute | solution.py:153
  125.1 1.2 copy-start.20
  136.8 0.8 copy-start.10
  137.6 8.0 %copy-start.25 = (bf16[1,24,128,128]{3,2,1,0:T(8,128)(2,1)S(1)}, bf16[1,24,128,128]{3,2,1,0:T(8,128)(2,1)}, u32[]{:S(2)}) copy-start(bf16[1,24,128,128]{3,2,1,0:T(8,128)(2,1)} %get-tuple-element.31) | copy-start | bytes 2359300
  138.3 15.3 %collective-permute-start.10 = (bf16[1,4,128,128]{3,2,1,0:T(8,128)(2,1)}, bf16[1,4,128,128]{3,2,1,0:T(8,128)(2,1)S(1)}, u32[]{:S(2)}, u32[]{:S(2)}) collective-permute-start(bf16[1,4,128,128]{3,2,1,0:T(8,128)(2,1)} %get-tuple-element.45), channel_id=1, source_target_pairs={{0,1},{1,2},{2,3},{3,4},{4,5},{5,6},{6,7},{8,9},{9,10},{10,11},{11... | collective-permute-start | bytes 393224 | tf_op jit(solution)/shard_map/ppermute | solution.py:152
  142.3 11.3 %collective-permute-start.11 = (bf16[1,4,128,128]{3,2,1,0:T(8,128)(2,1)}, bf16[1,4,128,128]{3,2,1,0:T(8,128)(2,1)}, u32[]{:S(2)}, u32[]{:S(2)}) collective-permute-start(bf16[1,4,128,128]{3,2,1,0:T(8,128)(2,1)} %get-tuple-element.46), channel_id=1, source_target_pairs={{1,0},{2,1},{3,2},{4,3},{5,4},{6,5},{7,6},{9,8},{10,9},{11,10},{12... | collective-permute-start | bytes 393224 | tf_op jit(solution)/shard_map/ppermute | solution.py:153
  143.6 10.0 %copy-start.11 = (bf16[1,16,128,128]{3,2,1,0:T(8,128)(2,1)S(1)}, bf16[1,16,128,128]{3,2,1,0:T(8,128)(2,1)}, u32[]{:S(2)}) copy-start(bf16[1,16,128,128]{3,2,1,0:T(8,128)(2,1)} %copy-done.10) | copy-start | bytes 1572868
  146.4 8.4 %copy-start.9 = (bf16[1,16,128,128]{3,2,1,0:T(8,128)(2,1)S(1)}, bf16[1,16,128,128]{3,2,1,0:T(8,128)(2,1)}, u32[]{:S(2)}) copy-start(bf16[1,16,128,128]{3,2,1,0:T(8,128)(2,1)} %copy-done.8) | copy-start | bytes 1572868
  146.4 8.4 %copy-start.14 = (bf16[1,24,128,128]{3,2,1,0:T(8,128)(2,1)S(1)}, bf16[1,24,128,128]{3,2,1,0:T(8,128)(2,1)}, u32[]{:S(2)}) copy-start(bf16[1,24,128,128]{3,2,1,0:T(8,128)(2,1)} %get-tuple-element.22) | copy-start | bytes 2359300
  146.4 8.4 %copy-start.26 = (bf16[1,16,128,128]{3,2,1,0:T(8,128)(2,1)S(1)}, bf16[1,16,128,128]{3,2,1,0:T(8,128)(2,1)}, u32[]{:S(2)}) copy-start(bf16[1,16,128,128]{3,2,1,0:T(8,128)(2,1)} %get-tuple-element.9) | copy-start | bytes 1572868
  153.6 1.3 copy-start.16
  153.6 1.4 copy-start.27
  159.7 1.0 copy-start.15
  160.7 5.7 %collective-permute-start.12 = (f32[1024,128]{1,0:T(8,128)S(1)}, f32[1024,128]{1,0:T(8,128)S(1)}, u32[]{:S(2)}, u32[]{:S(2)}) collective-permute-start(f32[1024,128]{1,0:T(8,128)S(1)} %constant_dynamic-slice_fusion.4), channel_id=1, source_target_pairs={{0,8},{8,0},{1,9},{9,1},{2,10},{10,2},{3,11},{11,3},{4,12},{12,4},... | collective-permute-start | bytes 1572872 | tf_op jit(solution)/shard_map/ppermute | solution.py:140
  167.6 15.0 %collective-permute-start.13 = (f32[512,128]{1,0:T(8,128)S(1)}, f32[512,128]{1,0:T(8,128)S(1)}, u32[]{:S(2)}, u32[]{:S(2)}) collective-permute-start(f32[512,128]{1,0:T(8,128)S(1)} %constant_dynamic-slice_fusion.3), channel_id=1, source_target_pairs={{0,16},{16,0},{32,48},{48,32},{1,17},{17,1},{33,49},{49,33},{2,18}... | collective-permute-start | bytes 786440 | tf_op jit(solution)/shard_map/ppermute | solution.py:140
  182.6 56.3 %copy-start.6 = (bf16[1,24,128,128]{3,2,1,0:T(8,128)(2,1)S(1)}, bf16[1,24,128,128]{3,2,1,0:T(8,128)(2,1)}, u32[]{:S(2)}) copy-start(bf16[1,24,128,128]{3,2,1,0:T(8,128)(2,1)} %get-tuple-element.30) | copy-start | bytes 2359300
  182.6 7.9 %collective-permute-start.14 = (f32[256,128]{1,0:T(8,128)S(1)}, f32[256,128]{1,0:T(8,128)S(1)}, u32[]{:S(2)}, u32[]{:S(2)}) collective-permute-start(f32[256,128]{1,0:T(8,128)S(1)} %constant_dynamic-slice_fusion.2), channel_id=1, source_target_pairs={{0,32},{16,48},{32,0},{48,16},{1,33},{17,49},{33,1},{49,17},{2,34}... | collective-permute-start | bytes 393224 | tf_op jit(solution)/shard_map/ppermute | solution.py:140
  190.6 3.5 %collective-permute-start.15 = (f32[128,128]{1,0:T(8,128)S(1)}, f32[128,128]{1,0:T(8,128)S(1)}, u32[]{:S(2)}, u32[]{:S(2)}) collective-permute-start(f32[128,128]{1,0:T(8,128)S(1)} %constant_dynamic-slice_fusion.1), channel_id=1, source_target_pairs={{0,64},{64,0},{128,192},{192,128},{1,65},{65,1},{129,193},{193,129... | collective-permute-start | bytes 196616 | tf_op jit(solution)/shard_map/ppermute | solution.py:140
  194.1 44.8 %copy-start.7 = (bf16[1,16,128,128]{3,2,1,0:T(8,128)(2,1)S(1)}, bf16[1,16,128,128]{3,2,1,0:T(8,128)(2,1)}, u32[]{:S(2)}) copy-start(bf16[1,16,128,128]{3,2,1,0:T(8,128)(2,1)} %add_convert_fusion.2) | copy-start | bytes 1572868
  194.1 4.4 %collective-permute-start.16 = (f32[64,128]{1,0:T(8,128)S(1)}, f32[64,128]{1,0:T(8,128)S(1)}, u32[]{:S(2)}, u32[]{:S(2)}) collective-permute-start(f32[64,128]{1,0:T(8,128)S(1)} %constant_dynamic-slice_fusion), channel_id=1, source_target_pairs={{0,128},{64,192},{128,0},{192,64},{1,129},{65,193},{129,1},{193,65... | collective-permute-start | bytes 98312 | tf_op jit(solution)/shard_map/ppermute | solution.py:140
  198.5 4.6 %collective-permute-start.17 = (f32[64,128]{1,0:T(8,128)S(1)}, f32[64,128]{1,0:T(8,128)S(1)}, u32[]{:S(2)}, u32[]{:S(2)}) collective-permute-start(f32[64,128]{1,0:T(8,128)S(1)} %dynamic-slice_add_fusion.4), channel_id=1, source_target_pairs={{0,128},{64,192},{128,0},{192,64},{1,129},{65,193},{129,1},{193,65... | collective-permute-start | bytes 98312 | tf_op jit(solution)/shard_map/ppermute | solution.py:143
  203.1 3.2 %collective-permute-start.18 = (f32[128,128]{1,0:T(8,128)S(1)}, f32[128,128]{1,0:T(8,128)S(1)}, u32[]{:S(2)}, u32[]{:S(2)}) collective-permute-start(f32[128,128]{1,0:T(8,128)S(1)} %maximum_select_fusion.4), channel_id=1, source_target_pairs={{0,64},{64,0},{128,192},{192,128},{1,65},{65,1},{129,193},{193,129... | collective-permute-start | bytes 196616 | tf_op jit(solution)/shard_map/ppermute | solution.py:143
  206.3 7.9 %collective-permute-start.19 = (f32[256,128]{1,0:T(8,128)S(1)}, f32[256,128]{1,0:T(8,128)S(1)}, u32[]{:S(2)}, u32[]{:S(2)}) collective-permute-start(f32[256,128]{1,0:T(8,128)S(1)} %maximum_select_fusion.3), channel_id=1, source_target_pairs={{0,32},{16,48},{32,0},{48,16},{1,33},{17,49},{33,1},{49,17},{2,34}... | collective-permute-start | bytes 393224 | tf_op jit(solution)/shard_map/ppermute | solution.py:143
  214.2 3.7 %copy-start.28 = (f32[512,128]{1,0:T(8,128)}, f32[512,128]{1,0:T(8,128)S(1)}, u32[]{:S(2)}) copy-start(f32[512,128]{1,0:T(8,128)S(1)} %maximum_select_fusion.2) | copy-start | bytes 786436
  214.2 13.1 %collective-permute-start.20 = (f32[512,128]{1,0:T(8,128)S(1)}, f32[512,128]{1,0:T(8,128)}, u32[]{:S(2)}, u32[]{:S(2)}) collective-permute-start(f32[512,128]{1,0:T(8,128)S(1)} %maximum_select_fusion.2), channel_id=1, source_target_pairs={{0,16},{16,0},{32,48},{48,32},{1,17},{17,1},{33,49},{49,33},{2,18}... | collective-permute-start | bytes 786440 | tf_op jit(solution)/shard_map/ppermute | solution.py:143
  228.6 12.9 %collective-permute-start.21 = (f32[1024,128]{1,0:T(8,128)S(1)}, f32[1024,128]{1,0:T(8,128)}, u32[]{:S(2)}, u32[]{:S(2)}) collective-permute-start(f32[1024,128]{1,0:T(8,128)S(1)} %maximum_select_fusion.1), channel_id=1, source_target_pairs={{0,8},{8,0},{1,9},{9,1},{2,10},{10,2},{3,11},{11,3},{4,12},{12,4},... | collective-permute-start | bytes 1572872 | tf_op jit(solution)/shard_map/ppermute | solution.py:143

commit v3 on v1

--- a/solution.py
+++ b/solution.py
@@ -121,7 +121,7 @@
     )
 
 
-HALVINGS = (("core", 1), ("zhi", 1), ("zhi", 2), ("y", 1), ("y", 2))
+HALVINGS = (("core", 1), ("y", 1), ("y", 2), ("zhi", 1), ("zhi", 2))
 
 
 def partner_bit(axis, mask):

time: 243 us -> 230 us (0.947)
  waiting for transfers between devices: 63.4 us -> 52.1 us
    ppermute x5, waiting for transfers between devices: 19.6 us -> 13.9 us  [reduce_shots(): rows = keep + lax.ppermute(send, axis, perm)]
    ppermute x5, waiting for transfers between devices: 18.2 us -> 12.6 us  [reduce_shots(): other = lax.ppermute(rows, axis, perm)]
where the time goes in v3:
time: 230 us; the launch traced here: 229 us
  starting transfers between devices  81.7 us (36%)
  other arithmetic  70.6 us (31%)
  waiting for transfers between devices  52.1 us (23%)
  local copies, waits for them, and re-layouts  22 us (10%)
    ppermute x8, starting transfers between devices, padded_2(): lax.ppermute(tail, axis, [(i, (i + 1) % count) for i in range(ends)])  32.1 us
    unnamed x7, other arithmetic  26.2 us
    ppermute x8, waiting for transfers between devices, padded_2(): lax.ppermute(head, axis, [((i + 1) % count, i) for i in range(ends)])  22.7 us
    ppermute x5, starting transfers between devices, reduce_shots(): rows = keep + lax.ppermute(send, axis, perm)  20.2 us
    ppermute x5, starting transfers between devices, reduce_shots(): other = lax.ppermute(rows, axis, perm)  19.1 us
    gather x4, local copies, waits for them, and re-layouts, record_rows(): picked = table[row_ids[0]].astype(jnp.float32)  16 us
    ppermute x5, waiting for transfers between devices, reduce_shots(): rows = keep + lax.ppermute(send, axis, perm)  13.9 us
    ppermute x5, waiting for transfers between devices, reduce_shots(): other = lax.ppermute(rows, axis, perm)  12.6 us
  transfers between devices with their start and end apart: 26, of which 20 were waited for; matrix products, arithmetic and copies ran while one was open for 11% of the time, Pallas kernels for 0%

profile of v3, /device:TPU:1, one launch (start us, length us, event | category | flops | bytes accessed | tf_op | source)
XLA Modules:
  0.0 228.7 jit_solution(18262212385149577868)
XLA Ops:
  0.7 1.2 slice_bitcast_fusion.1
  1.9 4.4 %collective-permute-start = (bf16[1,4,128,128]{3,2,1,0:T(8,128)(2,1)S(1)}, bf16[1,4,128,128]{3,2,1,0:T(8,128)(2,1)S(1)}, u32[]{:S(2)}, u32[]{:S(2)}) collective-permute-start(bf16[1,4,128,128]{3,2,1,0:T(8,128)(2,1)S(1)} %get-tuple-element.42), channel_id=1, source_target_pairs={{0,1},{1,2},{2,3},{3,4},{4,5},{5,6},{6,7},{8,9},{9,10},{10,11},{11... | collective-permute-start | bytes 393224 | tf_op jit(solution)/shard_map/ppermute | solution.py:33
  6.3 1.3 collective-permute-start.1
  7.7 4.0 %collective-permute-start.8 = (bf16[1,4,128,128]{3,2,1,0:T(8,128)(2,1)S(1)}, bf16[1,4,128,128]{3,2,1,0:T(8,128)(2,1)S(1)}, u32[]{:S(2)}, u32[]{:S(2)}) collective-permute-start(bf16[1,4,128,128]{3,2,1,0:T(8,128)(2,1)S(1)} %get-tuple-element.34), channel_id=1, source_target_pairs={{0,1},{1,2},{2,3},{3,4},{4,5},{5,6},{6,7},{8,9},{9,10},{10,11},{11... | collective-permute-start | bytes 393224 | tf_op jit(solution)/shard_map/ppermute | solution.py:33
  11.7 1.3 collective-permute-start.9
  14.9 3.0 %fusion.229 = (bf16[1,16,128,128]{3,2,1,0:T(8,128)(2,1)}, f32[1,16,128,128]{3,2,1,0:T(8,128)S(1)}) fusion(f32[1,24,128,128]{3,2,1,0:T(8,128)S(1)} %maximum_convert_fusion), kind=kLoop, calls=%fused_computation.485 | loop fusion | flops 7864320 | bytes 12582912 | tf_op jit(solution)/shard_map/convert_element_type | solution.py:167
  19.0 4.2 %collective-permute-start.2 = (bf16[1,4,128,128]{3,2,1,0:T(8,128)(2,1)S(1)}, bf16[1,4,128,128]{3,2,1,0:T(8,128)(2,1)S(1)}, u32[]{:S(2)}, u32[]{:S(2)}) collective-permute-start(bf16[1,4,128,128]{3,2,1,0:T(8,128)(2,1)S(1)} %get-tuple-element.40), channel_id=1, source_target_pairs={{0,1},{1,2},{2,3},{3,4},{4,5},{5,6},{6,7},{8,9},{9,10},{10,11},{11... | collective-permute-start | bytes 393224 | tf_op jit(solution)/shard_map/ppermute | solution.py:33
  23.2 1.3 collective-permute-start.3
  25.2 5.8 %collective-permute-done.3 = bf16[1,4,128,128]{3,2,1,0:T(8,128)(2,1)S(1)} collective-permute-done((bf16[1,4,128,128]{3,2,1,0:T(8,128)(2,1)S(1)}, bf16[1,4,128,128]{3,2,1,0:T(8,128)(2,1)S(1)}, u32[]{:S(2)}, u32[]{:S(2)}) %collective-permute-start.3) | collective-permute-done | bytes 131104 | tf_op jit(solution)/shard_map/ppermute | solution.py:35
  31.1 3.0 %fusion.227 = (bf16[1,16,128,128]{3,2,1,0:T(8,128)(2,1)}, f32[1,16,128,128]{3,2,1,0:T(8,128)S(1)}) fusion(f32[1,24,128,128]{3,2,1,0:T(8,128)S(1)} %maximum_convert_fusion.1), kind=kLoop, calls=%fused_computation.484 | loop fusion | flops 7864320 | bytes 12582912 | tf_op jit(solution)/shard_map/convert_element_type | solution.py:167
  35.2 3.2 %collective-permute-start.4 = (bf16[1,4,128,128]{3,2,1,0:T(8,128)(2,1)S(1)}, bf16[1,4,128,128]{3,2,1,0:T(8,128)(2,1)S(1)}, u32[]{:S(2)}, u32[]{:S(2)}) collective-permute-start(bf16[1,4,128,128]{3,2,1,0:T(8,128)(2,1)S(1)} %get-tuple-element.38), channel_id=1, source_target_pairs={{0,1},{1,2},{2,3},{3,4},{4,5},{5,6},{6,7},{8,9},{9,10},{10,11},{11... | collective-permute-start | bytes 393224 | tf_op jit(solution)/shard_map/ppermute | solution.py:33
  38.4 1.3 collective-permute-start.5
  40.4 4.6 %collective-permute-done.5 = bf16[1,4,128,128]{3,2,1,0:T(8,128)(2,1)S(1)} collective-permute-done((bf16[1,4,128,128]{3,2,1,0:T(8,128)(2,1)S(1)}, bf16[1,4,128,128]{3,2,1,0:T(8,128)(2,1)S(1)}, u32[]{:S(2)}, u32[]{:S(2)}) %collective-permute-start.5) | collective-permute-done | bytes 131104 | tf_op jit(solution)/shard_map/ppermute | solution.py:35
  45.1 3.1 %fusion.225 = (bf16[1,16,128,128]{3,2,1,0:T(8,128)(2,1)}, f32[1,16,128,128]{3,2,1,0:T(8,128)S(1)}) fusion(f32[1,24,128,128]{3,2,1,0:T(8,128)S(1)} %maximum_convert_fusion.2), kind=kLoop, calls=%fused_computation.483 | loop fusion | flops 7864320 | bytes 12582912 | tf_op jit(solution)/shard_map/convert_element_type | solution.py:167
  48.1 1.2 fusion.12
  49.3 4.4 %collective-permute-start.6 = (bf16[1,4,128,128]{3,2,1,0:T(8,128)(2,1)S(1)}, bf16[1,4,128,128]{3,2,1,0:T(8,128)(2,1)S(1)}, u32[]{:S(2)}, u32[]{:S(2)}) collective-permute-start(bf16[1,4,128,128]{3,2,1,0:T(8,128)(2,1)S(1)} %get-tuple-element.36), channel_id=1, source_target_pairs={{0,1},{1,2},{2,3},{3,4},{4,5},{5,6},{6,7},{8,9},{9,10},{10,11},{11... | collective-permute-start | bytes 393224 | tf_op jit(solution)/shard_map/ppermute | solution.py:33
  53.8 1.3 collective-permute-start.7
  55.1 3.2 %fusion.6 = f32[1,16,128,128]{3,2,1,0:T(8,128)} fusion(f32[1,24,128,128]{3,2,1,0:T(8,128)S(1)} %maximum_convert_fusion.4, bf16[2,1,16,128,128]{4,3,2,1,0:T(8,128)(2,1)S(1)} %copy-done.14, f32[16,128,128]{2,1,0:T(8,128)S(1)} %copy-done), kind=kLoop, calls=%fused_computation.162 | loop fusion | flops 9699328 | bytes 14155776 | tf_op jit(solution)/shard_map/add | solution.py:178
  58.3 3.2 %gather_fusion.3 = bf16[1024,128]{1,0:T(8,128)(2,1)S(1)} fusion(bf16[2048,128]{1,0:T(8,128)(2,1)S(1)} %bitcast.92, s32[1024]{0:T(1024)S(1)} %broadcast_clamp_fusion), kind=kCustom, calls=%fused_computation.3 | custom fusion | bytes 528384 | tf_op jit(solution)/shard_map/gather | solution.py:109
  61.5 4.3 %gather_fusion.2 = bf16[1024,128]{1,0:T(8,128)(2,1)} fusion(bf16[2048,128]{1,0:T(8,128)(2,1)S(1)} %bitcast.93, s32[1024]{0:T(1024)S(1)} %broadcast_clamp_fusion), kind=kCustom, calls=%fused_computation.2 | custom fusion | bytes 528384 | tf_op jit(solution)/shard_map/gather | solution.py:109
  65.7 4.3 %gather_fusion.1 = bf16[1024,128]{1,0:T(8,128)(2,1)} fusion(bf16[2048,128]{1,0:T(8,128)(2,1)S(1)} %bitcast.94, s32[1024]{0:T(1024)S(1)} %broadcast_clamp_fusion), kind=kCustom, calls=%fused_computation.1 | custom fusion | bytes 528384 | tf_op jit(solution)/shard_map/gather | solution.py:109
  70.1 3.0 %fusion.223 = (bf16[1,16,128,128]{3,2,1,0:T(8,128)(2,1)}, f32[1,16,128,128]{3,2,1,0:T(8,128)S(1)}) fusion(f32[1,24,128,128]{3,2,1,0:T(8,128)S(1)} %maximum_convert_fusion.3), kind=kLoop, calls=%fused_computation.482 | loop fusion | flops 7864320 | bytes 12582912 | tf_op jit(solution)/shard_map/convert_element_type | solution.py:167
  74.3 4.3 %gather_fusion = bf16[1024,128]{1,0:T(8,128)(2,1)} fusion(bf16[2048,128]{1,0:T(8,128)(2,1)S(1)} %bitcast.100, s32[1024]{0:T(1024)S(1)} %broadcast_clamp_fusion), kind=kCustom, calls=%fused_computation | custom fusion | bytes 528384 | tf_op jit(solution)/shard_map/gather | solution.py:109
  78.6 1.7 select_reduce_fusion
  80.3 6.6 %scatter_fusion = f32[262144]{0:T(1024)S(1)} fusion(f32[262144]{0:T(1024)S(1)} %bitcast.96, s32[1024]{0:T(1024)S(1)} %broadcast_select_fusion, f32[1024]{0:T(1024)S(1)} %bitcast.125), kind=kCustom, calls=%fused_computation.4 | custom fusion | flops 1024 | bytes 16384
  87.1 4.1 %collective-permute-start.10 = (bf16[1,4,128,128]{3,2,1,0:T(8,128)(2,1)S(1)}, bf16[1,4,128,128]{3,2,1,0:T(8,128)(2,1)S(1)}, u32[]{:S(2)}, u32[]{:S(2)}) collective-permute-start(bf16[1,4,128,128]{3,2,1,0:T(8,128)(2,1)S(1)} %get-tuple-element.32), channel_id=1, source_target_pairs={{0,1},{1,2},{2,3},{3,4},{4,5},{5,6},{6,7},{8,9},{9,10},{10,11},{11... | collective-permute-start | bytes 393224 | tf_op jit(solution)/shard_map/ppermute | solution.py:33
  91.2 1.3 collective-permute-start.11
  93.2 3.8 %collective-permute-done.11 = bf16[1,4,128,128]{3,2,1,0:T(8,128)(2,1)S(1)} collective-permute-done((bf16[1,4,128,128]{3,2,1,0:T(8,128)(2,1)S(1)}, bf16[1,4,128,128]{3,2,1,0:T(8,128)(2,1)S(1)}, u32[]{:S(2)}, u32[]{:S(2)}) %collective-permute-start.11) | collective-permute-done | bytes 131104 | tf_op jit(solution)/shard_map/ppermute | solution.py:35
  97.1 2.4 %fusion.7 = f32[1,16,128,128]{3,2,1,0:T(8,128)S(1)} fusion(bf16[1,16,128,128]{3,2,1,0:T(8,128)(2,1)S(1)} %bitcast.104, f32[1,24,128,128]{3,2,1,0:T(8,128)S(1)} %maximum_convert_fusion.5, f32[16,128,128]{2,1,0:T(8,128)S(1)} %copy-done, bf16[2,1,16,128,128]{4,3,2,1,0:T(8,128)(2,1)S(1)} %copy-done.15), kind=kLoop, calls=%fused_computation.163 | loop fusion | flops 9699328 | bytes 14155776 | tf_op jit(solution)/shard_map/add | solution.py:178
  99.5 6.5 %scatter_fusion.1 = f32[262144]{0:T(1024)S(1)} fusion(f32[262144]{0:T(1024)S(1)} %bitcast.98, s32[1024]{0:T(1024)S(1)} %broadcast_select_fusion, f32[1024]{0:T(1024)S(1)} %bitcast.124), kind=kCustom, calls=%fused_computation.5 | custom fusion | flops 1024 | bytes 16384
  106.1 5.6 %collective-permute-start.12 = (bf16[1,4,128,128]{3,2,1,0:T(8,128)(2,1)S(1)}, bf16[1,4,128,128]{3,2,1,0:T(8,128)(2,1)S(1)}, u32[]{:S(2)}, u32[]{:S(2)}) collective-permute-start(bf16[1,4,128,128]{3,2,1,0:T(8,128)(2,1)S(1)} %get-tuple-element.30), channel_id=1, source_target_pairs={{0,1},{1,2},{2,3},{3,4},{4,5},{5,6},{6,7},{8,9},{9,10},{10,11},{11... | collective-permute-start | bytes 393224 | tf_op jit(solution)/shard_map/ppermute | solution.py:33
  111.7 1.3 collective-permute-start.13
  113.7 4.5 %collective-permute-done.13 = bf16[1,4,128,128]{3,2,1,0:T(8,128)(2,1)S(1)} collective-permute-done((bf16[1,4,128,128]{3,2,1,0:T(8,128)(2,1)S(1)}, bf16[1,4,128,128]{3,2,1,0:T(8,128)(2,1)S(1)}, u32[]{:S(2)}, u32[]{:S(2)}) %collective-permute-start.13) | collective-permute-done | bytes 131104 | tf_op jit(solution)/shard_map/ppermute | solution.py:35
  118.3 2.4 %fusion.14 = f32[1,16,128,128]{3,2,1,0:T(8,128)S(1)} fusion(bf16[1,16,128,128]{3,2,1,0:T(8,128)(2,1)S(1)} %bitcast.105, bf16[1,16,128,128]{3,2,1,0:T(8,128)(2,1)S(1)} %bitcast.109, f32[1,24,128,128]{3,2,1,0:T(8,128)S(1)} %maximum_convert_fusion.6, f32[16,128,128]{2,1,0:T(8,128)S(1)} %copy-done), kind=kLoop, calls=%fused_computation.170 | loop fusion | flops 9699328 | bytes 14155776 | tf_op jit(solution)/shard_map/add | solution.py:178
  120.7 6.5 %scatter_fusion.2 = f32[262144]{0:T(1024)S(1)} fusion(f32[262144]{0:T(1024)S(1)} %bitcast.99, s32[1024]{0:T(1024)S(1)} %broadcast_select_fusion, f32[1024]{0:T(1024)S(1)} %bitcast.123), kind=kCustom, calls=%fused_computation.6 | custom fusion | flops 1024 | bytes 16384
  128.0 2.1 collective-permute-start.14
  130.2 1.3 collective-permute-start.15
  132.1 4.1 %collective-permute-done.15 = bf16[1,4,128,128]{3,2,1,0:T(8,128)(2,1)S(1)} collective-permute-done((bf16[1,4,128,128]{3,2,1,0:T(8,128)(2,1)S(1)}, bf16[1,4,128,128]{3,2,1,0:T(8,128)(2,1)S(1)}, u32[]{:S(2)}, u32[]{:S(2)}) %collective-permute-start.15) | collective-permute-done | bytes 131104 | tf_op jit(solution)/shard_map/ppermute | solution.py:35
  136.2 1.2 maximum_convert_fusion.7
  137.4 3.3 %fusion.16 = f32[1,16,128,128]{3,2,1,0:T(8,128)S(1)} fusion(bf16[1,16,128,128]{3,2,1,0:T(8,128)(2,1)} %bitcast.110, bf16[1,16,128,128]{3,2,1,0:T(8,128)(2,1)S(1)} %bitcast.114, f32[1,24,128,128]{3,2,1,0:T(8,128)S(1)} %maximum_convert_fusion.7, f32[16,128,128]{2,1,0:T(8,128)S(1)} %copy-done), kind=kLoop, calls=%fused_computation.172 | loop fusion | flops 9699328 | bytes 14155776 | tf_op jit(solution)/shard_map/add | solution.py:178
  140.7 6.5 %scatter_fusion.3 = f32[262144]{0:T(1024)S(1)} fusion(f32[262144]{0:T(1024)S(1)} %bitcast.97, s32[1024]{0:T(1024)S(1)} %broadcast_select_fusion, f32[1024]{0:T(1024)S(1)} %bitcast.122), kind=kCustom, calls=%fused_computation.7 | custom fusion | flops 1024 | bytes 16384
  148.7 2.1 fusion.9
  151.7 6.2 %collective-permute-start.16 = (f32[1024,128]{1,0:T(8,128)}, f32[1024,128]{1,0:T(8,128)}, u32[]{:S(2)}, u32[]{:S(2)}) collective-permute-start(f32[1024,128]{1,0:T(8,128)} %constant_dynamic-slice_fusion.4), channel_id=1, source_target_pairs={{0,8},{8,0},{1,9},{9,1},{2,10},{10,2},{3,11},{11,3},{4,12},{12,4},... | collective-permute-start | bytes 1572872 | tf_op jit(solution)/shard_map/ppermute | solution.py:140
  157.9 1.9 collective-permute-done.16
  161.7 1.4 collective-permute-start.17
  163.1 6.2 %collective-permute-done.17 = f32[512,128]{1,0:T(8,128)S(1)} collective-permute-done((f32[512,128]{1,0:T(8,128)S(1)}, f32[512,128]{1,0:T(8,128)S(1)}, u32[]{:S(2)}, u32[]{:S(2)}) %collective-permute-start.17) | collective-permute-done | bytes 262176 | tf_op jit(solution)/shard_map/ppermute | solution.py:140
  170.3 3.2 %collective-permute-start.18 = (f32[256,128]{1,0:T(8,128)S(1)}, f32[256,128]{1,0:T(8,128)}, u32[]{:S(2)}, u32[]{:S(2)}) collective-permute-start(f32[256,128]{1,0:T(8,128)S(1)} %constant_dynamic-slice_fusion.2), channel_id=1, source_target_pairs={{0,128},{64,192},{128,0},{192,64},{1,129},{65,193},{129,1},{193,65... | collective-permute-start | bytes 393224 | tf_op jit(solution)/shard_map/ppermute | solution.py:140
  173.5 2.5 %collective-permute-done.18 = f32[256,128]{1,0:T(8,128)} collective-permute-done((f32[256,128]{1,0:T(8,128)S(1)}, f32[256,128]{1,0:T(8,128)}, u32[]{:S(2)}, u32[]{:S(2)}) %collective-permute-start.18) | collective-permute-done | bytes 131104 | tf_op jit(solution)/shard_map/ppermute | solution.py:140
  177.0 3.1 %collective-permute-start.19 = (f32[128,128]{1,0:T(8,128)S(1)}, f32[128,128]{1,0:T(8,128)S(1)}, u32[]{:S(2)}, u32[]{:S(2)}) collective-permute-start(f32[128,128]{1,0:T(8,128)S(1)} %constant_dynamic-slice_fusion.1), channel_id=1, source_target_pairs={{0,16},{16,0},{32,48},{48,32},{1,17},{17,1},{33,49},{49,33},{2,18}... | collective-permute-start | bytes 196616 | tf_op jit(solution)/shard_map/ppermute | solution.py:140
  180.1 1.7 collective-permute-done.19
  181.8 6.4 %collective-permute-start.20 = (f32[64,128]{1,0:T(8,128)S(1)}, f32[64,128]{1,0:T(8,128)S(1)}, u32[]{:S(2)}, u32[]{:S(2)}) collective-permute-start(f32[64,128]{1,0:T(8,128)S(1)} %constant_dynamic-slice_fusion), channel_id=1, source_target_pairs={{0,32},{16,48},{32,0},{48,16},{1,33},{17,49},{33,1},{49,17},{2,34}... | collective-permute-start | bytes 98312 | tf_op jit(solution)/shard_map/ppermute | solution.py:140
  188.1 1.7 collective-permute-done.20
  189.8 5.0 %collective-permute-start.21 = (f32[64,128]{1,0:T(8,128)S(1)}, f32[64,128]{1,0:T(8,128)S(1)}, u32[]{:S(2)}, u32[]{:S(2)}) collective-permute-start(f32[64,128]{1,0:T(8,128)S(1)} %dynamic-slice_add_fusion.4), channel_id=1, source_target_pairs={{0,32},{16,48},{32,0},{48,16},{1,33},{17,49},{33,1},{49,17},{2,34}... | collective-permute-start | bytes 98312 | tf_op jit(solution)/shard_map/ppermute | solution.py:143
  194.8 1.7 collective-permute-done.21
  196.5 1.2 collective-permute-start.22
  197.7 3.2 %collective-permute-done.22 = f32[128,128]{1,0:T(8,128)S(1)} collective-permute-done((f32[128,128]{1,0:T(8,128)S(1)}, f32[128,128]{1,0:T(8,128)S(1)}, u32[]{:S(2)}, u32[]{:S(2)}) %collective-permute-start.22) | collective-permute-done | bytes 65568 | tf_op jit(solution)/shard_map/ppermute | solution.py:143
  200.9 3.0 %collective-permute-start.23 = (f32[256,128]{1,0:T(8,128)S(1)}, f32[256,128]{1,0:T(8,128)}, u32[]{:S(2)}, u32[]{:S(2)}) collective-permute-start(f32[256,128]{1,0:T(8,128)S(1)} %maximum_select_fusion.3), channel_id=1, source_target_pairs={{0,128},{64,192},{128,0},{192,64},{1,129},{65,193},{129,1},{193,65... | collective-permute-start | bytes 393224 | tf_op jit(solution)/shard_map/ppermute | solution.py:143
  203.9 2.5 %collective-permute-done.23 = f32[256,128]{1,0:T(8,128)} collective-permute-done((f32[256,128]{1,0:T(8,128)S(1)}, f32[256,128]{1,0:T(8,128)}, u32[]{:S(2)}, u32[]{:S(2)}) %collective-permute-start.23) | collective-permute-done | bytes 131104 | tf_op jit(solution)/shard_map/ppermute | solution.py:143
  207.4 1.5 collective-permute-start.24
  208.9 4.9 %collective-permute-done.24 = f32[512,128]{1,0:T(8,128)} collective-permute-done((f32[512,128]{1,0:T(8,128)S(1)}, f32[512,128]{1,0:T(8,128)}, u32[]{:S(2)}, u32[]{:S(2)}) %collective-permute-start.24) | collective-permute-done | bytes 262176 | tf_op jit(solution)/shard_map/ppermute | solution.py:143
  213.8 1.9 maximum_select_fusion.1
  215.7 8.3 %collective-permute-start.25 = (f32[1024,128]{1,0:T(8,128)}, f32[1024,128]{1,0:T(8,128)}, u32[]{:S(2)}, u32[]{:S(2)}) collective-permute-start(f32[1024,128]{1,0:T(8,128)} %maximum_select_fusion.1), channel_id=1, source_target_pairs={{0,8},{8,0},{1,9},{9,1},{2,10},{10,2},{3,11},{11,3},{4,12},{12,4},... | collective-permute-start | bytes 1572872 | tf_op jit(solution)/shard_map/ppermute | solution.py:143
  224.0 1.5 pad_maximum_fusion
  225.9 1.7 fusion.213
  (104 shorter events, 18.0 us)
Async XLA Ops:
  0.6 12.5 %copy-start.21 = (s32[2]{0:T(128)S(1)}, s32[2]{0:T(128)}, u32[]{:S(2)}) copy-start(s32[2]{0:T(128)} %constant.355) | copy-start | bytes 28
  0.6 12.6 %copy-start.22 = (s32[2]{0:T(128)S(1)}, s32[2]{0:T(128)}, u32[]{:S(2)}) copy-start(s32[2]{0:T(128)} %constant.358) | copy-start | bytes 28
  0.7 6.9 %copy-start.13 = (bf16[2,1,16,128,128]{4,3,2,1,0:T(8,128)(2,1)S(1)}, bf16[2,1,16,128,128]{4,3,2,1,0:T(8,128)(2,1)}, u32[]{:S(2)}) copy-start(bf16[2,1,16,128,128]{4,3,2,1,0:T(8,128)(2,1)} %param.8) | copy-start | bytes 3145732
  0.7 12.3 %copy-start.19 = (s32[1,1024]{1,0:T(1,128)S(1)}, s32[1,1024]{1,0:T(1,128)}, u32[]{:S(2)}) copy-start(s32[1,1024]{1,0:T(1,128)} %param.12) | copy-start | bytes 12292
  0.7 13.3 %copy-start.20 = (f32[1,4]{1,0:T(1,128)S(1)}, f32[1,4]{1,0:T(1,128)}, u32[]{:S(2)}) copy-start(f32[1,4]{1,0:T(1,128)} %param.11) | copy-start | bytes 52
  1.9 12.8 %collective-permute-start = (bf16[1,4,128,128]{3,2,1,0:T(8,128)(2,1)S(1)}, bf16[1,4,128,128]{3,2,1,0:T(8,128)(2,1)S(1)}, u32[]{:S(2)}, u32[]{:S(2)}) collective-permute-start(bf16[1,4,128,128]{3,2,1,0:T(8,128)(2,1)S(1)} %get-tuple-element.42), channel_id=1, source_target_pairs={{0,1},{1,2},{2,3},{3,4},{4,5},{5,6},{6,7},{8,9},{9,10},{10,11},{11... | collective-permute-start | bytes 393224 | tf_op jit(solution)/shard_map/ppermute | solution.py:33
  6.3 8.4 %collective-permute-start.1 = (bf16[1,4,128,128]{3,2,1,0:T(8,128)(2,1)S(1)}, bf16[1,4,128,128]{3,2,1,0:T(8,128)(2,1)S(1)}, u32[]{:S(2)}, u32[]{:S(2)}) collective-permute-start(bf16[1,4,128,128]{3,2,1,0:T(8,128)(2,1)S(1)} %get-tuple-element.43), channel_id=1, source_target_pairs={{1,0},{2,1},{3,2},{4,3},{5,4},{6,5},{7,6},{9,8},{10,9},{11,10},{12... | collective-permute-start | bytes 393224 | tf_op jit(solution)/shard_map/ppermute | solution.py:35
  7.7 32.1 %collective-permute-start.8 = (bf16[1,4,128,128]{3,2,1,0:T(8,128)(2,1)S(1)}, bf16[1,4,128,128]{3,2,1,0:T(8,128)(2,1)S(1)}, u32[]{:S(2)}, u32[]{:S(2)}) collective-permute-start(bf16[1,4,128,128]{3,2,1,0:T(8,128)(2,1)S(1)} %get-tuple-element.34), channel_id=1, source_target_pairs={{0,1},{1,2},{2,3},{3,4},{4,5},{5,6},{6,7},{8,9},{9,10},{10,11},{11... | collective-permute-start | bytes 393224 | tf_op jit(solution)/shard_map/ppermute | solution.py:33
  11.7 28.1 %collective-permute-start.9 = (bf16[1,4,128,128]{3,2,1,0:T(8,128)(2,1)S(1)}, bf16[1,4,128,128]{3,2,1,0:T(8,128)(2,1)S(1)}, u32[]{:S(2)}, u32[]{:S(2)}) collective-permute-start(bf16[1,4,128,128]{3,2,1,0:T(8,128)(2,1)S(1)} %get-tuple-element.35), channel_id=1, source_target_pairs={{1,0},{2,1},{3,2},{4,3},{5,4},{6,5},{7,6},{9,8},{10,9},{11,10},{12... | collective-permute-start | bytes 393224 | tf_op jit(solution)/shard_map/ppermute | solution.py:35
  14.8 3.1 %copy-start = (f32[16,128,128]{2,1,0:T(8,128)S(1)}, f32[16,128,128]{2,1,0:T(8,128)}, u32[]{:S(2)}) copy-start(f32[16,128,128]{2,1,0:T(8,128)} %param.9) | copy-start | bytes 3145732
  14.8 3.1 %copy-start.16 = (bf16[2,1,16,128,128]{4,3,2,1,0:T(8,128)(2,1)S(1)}, bf16[2,1,16,128,128]{4,3,2,1,0:T(8,128)(2,1)}, u32[]{:S(2)}) copy-start(bf16[2,1,16,128,128]{4,3,2,1,0:T(8,128)(2,1)} %param.7) | copy-start | bytes 3145732
  19.0 6.1 %collective-permute-start.2 = (bf16[1,4,128,128]{3,2,1,0:T(8,128)(2,1)S(1)}, bf16[1,4,128,128]{3,2,1,0:T(8,128)(2,1)S(1)}, u32[]{:S(2)}, u32[]{:S(2)}) collective-permute-start(bf16[1,4,128,128]{3,2,1,0:T(8,128)(2,1)S(1)} %get-tuple-element.40), channel_id=1, source_target_pairs={{0,1},{1,2},{2,3},{3,4},{4,5},{5,6},{6,7},{8,9},{9,10},{10,11},{11... | collective-permute-start | bytes 393224 | tf_op jit(solution)/shard_map/ppermute | solution.py:33
  23.2 7.7 %collective-permute-start.3 = (bf16[1,4,128,128]{3,2,1,0:T(8,128)(2,1)S(1)}, bf16[1,4,128,128]{3,2,1,0:T(8,128)(2,1)S(1)}, u32[]{:S(2)}, u32[]{:S(2)}) collective-permute-start(bf16[1,4,128,128]{3,2,1,0:T(8,128)(2,1)S(1)} %get-tuple-element.41), channel_id=1, source_target_pairs={{1,0},{2,1},{3,2},{4,3},{5,4},{6,5},{7,6},{9,8},{10,9},{11,10},{12... | collective-permute-start | bytes 393224 | tf_op jit(solution)/shard_map/ppermute | solution.py:35
  35.2 5.1 %collective-permute-start.4 = (bf16[1,4,128,128]{3,2,1,0:T(8,128)(2,1)S(1)}, bf16[1,4,128,128]{3,2,1,0:T(8,128)(2,1)S(1)}, u32[]{:S(2)}, u32[]{:S(2)}) collective-permute-start(bf16[1,4,128,128]{3,2,1,0:T(8,128)(2,1)S(1)} %get-tuple-element.38), channel_id=1, source_target_pairs={{0,1},{1,2},{2,3},{3,4},{4,5},{5,6},{6,7},{8,9},{9,10},{10,11},{11... | collective-permute-start | bytes 393224 | tf_op jit(solution)/shard_map/ppermute | solution.py:33
  38.4 6.5 %collective-permute-start.5 = (bf16[1,4,128,128]{3,2,1,0:T(8,128)(2,1)S(1)}, bf16[1,4,128,128]{3,2,1,0:T(8,128)(2,1)S(1)}, u32[]{:S(2)}, u32[]{:S(2)}) collective-permute-start(bf16[1,4,128,128]{3,2,1,0:T(8,128)(2,1)S(1)} %get-tuple-element.39), channel_id=1, source_target_pairs={{1,0},{2,1},{3,2},{4,3},{5,4},{6,5},{7,6},{9,8},{10,9},{11,10},{12... | collective-permute-start | bytes 393224 | tf_op jit(solution)/shard_map/ppermute | solution.py:35
  48.1 7.0 %copy-start.14 = (bf16[2,1,16,128,128]{4,3,2,1,0:T(8,128)(2,1)S(1)}, bf16[2,1,16,128,128]{4,3,2,1,0:T(8,128)(2,1)}, u32[]{:S(2)}) copy-start(bf16[2,1,16,128,128]{4,3,2,1,0:T(8,128)(2,1)} %param.8) | copy-start | bytes 3145732
  49.3 20.7 %collective-permute-start.6 = (bf16[1,4,128,128]{3,2,1,0:T(8,128)(2,1)S(1)}, bf16[1,4,128,128]{3,2,1,0:T(8,128)(2,1)S(1)}, u32[]{:S(2)}, u32[]{:S(2)}) collective-permute-start(bf16[1,4,128,128]{3,2,1,0:T(8,128)(2,1)S(1)} %get-tuple-element.36), channel_id=1, source_target_pairs={{0,1},{1,2},{2,3},{3,4},{4,5},{5,6},{6,7},{8,9},{9,10},{10,11},{11... | collective-permute-start | bytes 393224 | tf_op jit(solution)/shard_map/ppermute | solution.py:33
  53.8 16.2 %collective-permute-start.7 = (bf16[1,4,128,128]{3,2,1,0:T(8,128)(2,1)S(1)}, bf16[1,4,128,128]{3,2,1,0:T(8,128)(2,1)S(1)}, u32[]{:S(2)}, u32[]{:S(2)}) collective-permute-start(bf16[1,4,128,128]{3,2,1,0:T(8,128)(2,1)S(1)} %get-tuple-element.37), channel_id=1, source_target_pairs={{1,0},{2,1},{3,2},{4,3},{5,4},{6,5},{7,6},{9,8},{10,9},{11,10},{12... | collective-permute-start | bytes 393224 | tf_op jit(solution)/shard_map/ppermute | solution.py:35
  74.3 6.0 %copy-start.18 = (f32[1,4,1024]{2,1,0:T(4,128)S(1)}, f32[1,4,1024]{2,1,0:T(4,128)}, u32[]{:S(2)}) copy-start(f32[1,4,1024]{2,1,0:T(4,128)} %param.13) | copy-start | bytes 49156
  74.3 6.0 %copy-start.1 = (f32[1,16,128,128]{3,2,1,0:T(8,128)S(1)}, f32[1,16,128,128]{3,2,1,0:T(8,128)}, u32[]{:S(2)}) copy-start(f32[1,16,128,128]{3,2,1,0:T(8,128)} %fusion.6) | copy-start | bytes 3145732
  87.1 12.4 %copy-start.2 = (bf16[262144]{0:T(1024)(128)(2,1)}, bf16[262144]{0:T(1024)(128)(2,1)S(1)}, u32[]{:S(2)}) copy-start(bf16[262144]{0:T(1024)(128)(2,1)S(1)} %convert_element_type.468) | copy-start | bytes 1572868
  87.1 10.0 %copy-start.15 = (bf16[2,1,16,128,128]{4,3,2,1,0:T(8,128)(2,1)S(1)}, bf16[2,1,16,128,128]{4,3,2,1,0:T(8,128)(2,1)}, u32[]{:S(2)}) copy-start(bf16[2,1,16,128,128]{4,3,2,1,0:T(8,128)(2,1)} %param.8) | copy-start | bytes 3145732
  87.1 6.1 %collective-permute-start.10 = (bf16[1,4,128,128]{3,2,1,0:T(8,128)(2,1)S(1)}, bf16[1,4,128,128]{3,2,1,0:T(8,128)(2,1)S(1)}, u32[]{:S(2)}, u32[]{:S(2)}) collective-permute-start(bf16[1,4,128,128]{3,2,1,0:T(8,128)(2,1)S(1)} %get-tuple-element.32), channel_id=1, source_target_pairs={{0,1},{1,2},{2,3},{3,4},{4,5},{5,6},{6,7},{8,9},{9,10},{10,11},{11... | collective-permute-start | bytes 393224 | tf_op jit(solution)/shard_map/ppermute | solution.py:33
  91.2 5.7 %collective-permute-start.11 = (bf16[1,4,128,128]{3,2,1,0:T(8,128)(2,1)S(1)}, bf16[1,4,128,128]{3,2,1,0:T(8,128)(2,1)S(1)}, u32[]{:S(2)}, u32[]{:S(2)}) collective-permute-start(bf16[1,4,128,128]{3,2,1,0:T(8,128)(2,1)S(1)} %get-tuple-element.33), channel_id=1, source_target_pairs={{1,0},{2,1},{3,2},{4,3},{5,4},{6,5},{7,6},{9,8},{10,9},{11,10},{12... | collective-permute-start | bytes 393224 | tf_op jit(solution)/shard_map/ppermute | solution.py:35
  106.0 14.7 %copy-start.5 = (bf16[262144]{0:T(1024)(128)(2,1)}, bf16[262144]{0:T(1024)(128)(2,1)S(1)}, u32[]{:S(2)}) copy-start(bf16[262144]{0:T(1024)(128)(2,1)S(1)} %convert_element_type.469) | copy-start | bytes 1572868
  106.0 12.2 %copy-start.3 = (bf16[262144]{0:T(1024)(128)(2,1)S(1)}, bf16[262144]{0:T(1024)(128)(2,1)}, u32[]{:S(2)}) copy-start(bf16[262144]{0:T(1024)(128)(2,1)} %copy-done.2) | copy-start | bytes 1572868
  106.1 7.6 %collective-permute-start.12 = (bf16[1,4,128,128]{3,2,1,0:T(8,128)(2,1)S(1)}, bf16[1,4,128,128]{3,2,1,0:T(8,128)(2,1)S(1)}, u32[]{:S(2)}, u32[]{:S(2)}) collective-permute-start(bf16[1,4,128,128]{3,2,1,0:T(8,128)(2,1)S(1)} %get-tuple-element.30), channel_id=1, source_target_pairs={{0,1},{1,2},{2,3},{3,4},{4,5},{5,6},{6,7},{8,9},{9,10},{10,11},{11... | collective-permute-start | bytes 393224 | tf_op jit(solution)/shard_map/ppermute | solution.py:33
  111.7 6.4 %collective-permute-start.13 = (bf16[1,4,128,128]{3,2,1,0:T(8,128)(2,1)S(1)}, bf16[1,4,128,128]{3,2,1,0:T(8,128)(2,1)S(1)}, u32[]{:S(2)}, u32[]{:S(2)}) collective-permute-start(bf16[1,4,128,128]{3,2,1,0:T(8,128)(2,1)S(1)} %get-tuple-element.31), channel_id=1, source_target_pairs={{1,0},{2,1},{3,2},{4,3},{5,4},{6,5},{7,6},{9,8},{10,9},{11,10},{12... | collective-permute-start | bytes 393224 | tf_op jit(solution)/shard_map/ppermute | solution.py:35
  127.2 0.8 copy-start.7
  128.0 4.1 %collective-permute-start.14 = (bf16[1,4,128,128]{3,2,1,0:T(8,128)(2,1)S(1)}, bf16[1,4,128,128]{3,2,1,0:T(8,128)(2,1)S(1)}, u32[]{:S(2)}, u32[]{:S(2)}) collective-permute-start(bf16[1,4,128,128]{3,2,1,0:T(8,128)(2,1)S(1)} %get-tuple-element.28), channel_id=1, source_target_pairs={{0,1},{1,2},{2,3},{3,4},{4,5},{5,6},{6,7},{8,9},{9,10},{10,11},{11... | collective-permute-start | bytes 393224 | tf_op jit(solution)/shard_map/ppermute | solution.py:33
  130.2 6.0 %collective-permute-start.15 = (bf16[1,4,128,128]{3,2,1,0:T(8,128)(2,1)S(1)}, bf16[1,4,128,128]{3,2,1,0:T(8,128)(2,1)S(1)}, u32[]{:S(2)}, u32[]{:S(2)}) collective-permute-start(bf16[1,4,128,128]{3,2,1,0:T(8,128)(2,1)S(1)} %get-tuple-element.29), channel_id=1, source_target_pairs={{1,0},{2,1},{3,2},{4,3},{5,4},{6,5},{7,6},{9,8},{10,9},{11,10},{12... | collective-permute-start | bytes 393224 | tf_op jit(solution)/shard_map/ppermute | solution.py:35
  131.5 5.9 %copy-start.8 = (bf16[262144]{0:T(1024)(128)(2,1)S(1)}, bf16[262144]{0:T(1024)(128)(2,1)}, u32[]{:S(2)}) copy-start(bf16[262144]{0:T(1024)(128)(2,1)} %copy-done.7) | copy-start | bytes 1572868
  147.2 1.2 copy-start.4
  147.2 1.4 copy-start.6
  147.2 1.5 copy-start.9
  147.3 3.6 %copy-start.11 = (bf16[262144]{0:T(1024)(128)(2,1)}, bf16[262144]{0:T(1024)(128)(2,1)S(1)}, u32[]{:S(2)}) copy-start(bf16[262144]{0:T(1024)(128)(2,1)S(1)} %convert_element_type.471) | copy-start | bytes 1572868
  151.7 8.1 %collective-permute-start.16 = (f32[1024,128]{1,0:T(8,128)}, f32[1024,128]{1,0:T(8,128)}, u32[]{:S(2)}, u32[]{:S(2)}) collective-permute-start(f32[1024,128]{1,0:T(8,128)} %constant_dynamic-slice_fusion.4), channel_id=1, source_target_pairs={{0,8},{8,0},{1,9},{9,1},{2,10},{10,2},{3,11},{11,3},{4,12},{12,4},... | collective-permute-start | bytes 1572872 | tf_op jit(solution)/shard_map/ppermute | solution.py:140
  160.9 0.8 copy-start.17
  161.7 7.6 %collective-permute-start.17 = (f32[512,128]{1,0:T(8,128)S(1)}, f32[512,128]{1,0:T(8,128)S(1)}, u32[]{:S(2)}, u32[]{:S(2)}) collective-permute-start(f32[512,128]{1,0:T(8,128)S(1)} %constant_dynamic-slice_fusion.3), channel_id=1, source_target_pairs={{0,64},{64,0},{128,192},{192,128},{1,65},{65,1},{129,193},{193,129... | collective-permute-start | bytes 786440 | tf_op jit(solution)/shard_map/ppermute | solution.py:140
  170.3 53.7 %copy-start.10 = (bf16[262144]{0:T(1024)(128)(2,1)S(1)}, bf16[262144]{0:T(1024)(128)(2,1)}, u32[]{:S(2)}) copy-start(bf16[262144]{0:T(1024)(128)(2,1)} %copy-done.7) | copy-start | bytes 1572868
  170.3 53.7 %copy-start.12 = (bf16[262144]{0:T(1024)(128)(2,1)S(1)}, bf16[262144]{0:T(1024)(128)(2,1)}, u32[]{:S(2)}) copy-start(bf16[262144]{0:T(1024)(128)(2,1)} %copy-done.11) | copy-start | bytes 1572868
  170.3 5.7 %collective-permute-start.18 = (f32[256,128]{1,0:T(8,128)S(1)}, f32[256,128]{1,0:T(8,128)}, u32[]{:S(2)}, u32[]{:S(2)}) collective-permute-start(f32[256,128]{1,0:T(8,128)S(1)} %constant_dynamic-slice_fusion.2), channel_id=1, source_target_pairs={{0,128},{64,192},{128,0},{192,64},{1,129},{65,193},{129,1},{193,65... | collective-permute-start | bytes 393224 | tf_op jit(solution)/shard_map/ppermute | solution.py:140
  177.0 4.7 %collective-permute-start.19 = (f32[128,128]{1,0:T(8,128)S(1)}, f32[128,128]{1,0:T(8,128)S(1)}, u32[]{:S(2)}, u32[]{:S(2)}) collective-permute-start(f32[128,128]{1,0:T(8,128)S(1)} %constant_dynamic-slice_fusion.1), channel_id=1, source_target_pairs={{0,16},{16,0},{32,48},{48,32},{1,17},{17,1},{33,49},{49,33},{2,18}... | collective-permute-start | bytes 196616 | tf_op jit(solution)/shard_map/ppermute | solution.py:140
  181.8 8.0 %collective-permute-start.20 = (f32[64,128]{1,0:T(8,128)S(1)}, f32[64,128]{1,0:T(8,128)S(1)}, u32[]{:S(2)}, u32[]{:S(2)}) collective-permute-start(f32[64,128]{1,0:T(8,128)S(1)} %constant_dynamic-slice_fusion), channel_id=1, source_target_pairs={{0,32},{16,48},{32,0},{48,16},{1,33},{17,49},{33,1},{49,17},{2,34}... | collective-permute-start | bytes 98312 | tf_op jit(solution)/shard_map/ppermute | solution.py:140
  189.8 6.7 %collective-permute-start.21 = (f32[64,128]{1,0:T(8,128)S(1)}, f32[64,128]{1,0:T(8,128)S(1)}, u32[]{:S(2)}, u32[]{:S(2)}) collective-permute-start(f32[64,128]{1,0:T(8,128)S(1)} %dynamic-slice_add_fusion.4), channel_id=1, source_target_pairs={{0,32},{16,48},{32,0},{48,16},{1,33},{17,49},{33,1},{49,17},{2,34}... | collective-permute-start | bytes 98312 | tf_op jit(solution)/shard_map/ppermute | solution.py:143
  196.5 4.4 %collective-permute-start.22 = (f32[128,128]{1,0:T(8,128)S(1)}, f32[128,128]{1,0:T(8,128)S(1)}, u32[]{:S(2)}, u32[]{:S(2)}) collective-permute-start(f32[128,128]{1,0:T(8,128)S(1)} %maximum_select_fusion.4), channel_id=1, source_target_pairs={{0,16},{16,0},{32,48},{48,32},{1,17},{17,1},{33,49},{49,33},{2,18}... | collective-permute-start | bytes 196616 | tf_op jit(solution)/shard_map/ppermute | solution.py:143
  200.9 5.5 %collective-permute-start.23 = (f32[256,128]{1,0:T(8,128)S(1)}, f32[256,128]{1,0:T(8,128)}, u32[]{:S(2)}, u32[]{:S(2)}) collective-permute-start(f32[256,128]{1,0:T(8,128)S(1)} %maximum_select_fusion.3), channel_id=1, source_target_pairs={{0,128},{64,192},{128,0},{192,64},{1,129},{65,193},{129,1},{193,65... | collective-permute-start | bytes 393224 | tf_op jit(solution)/shard_map/ppermute | solution.py:143
  207.4 6.4 %collective-permute-start.24 = (f32[512,128]{1,0:T(8,128)S(1)}, f32[512,128]{1,0:T(8,128)}, u32[]{:S(2)}, u32[]{:S(2)}) collective-permute-start(f32[512,128]{1,0:T(8,128)S(1)} %maximum_select_fusion.2), channel_id=1, source_target_pairs={{0,64},{64,0},{128,192},{192,128},{1,65},{65,1},{129,193},{193,129... | collective-permute-start | bytes 786440 | tf_op jit(solution)/shard_map/ppermute | solution.py:143
  215.7 10.2 %collective-permute-start.25 = (f32[1024,128]{1,0:T(8,128)}, f32[1024,128]{1,0:T(8,128)}, u32[]{:S(2)}, u32[]{:S(2)}) collective-permute-start(f32[1024,128]{1,0:T(8,128)} %maximum_select_fusion.1), channel_id=1, source_target_pairs={{0,8},{8,0},{1,9},{9,1},{2,10},{10,2},{3,11},{11,3},{4,12},{12,4},... | collective-permute-start | bytes 1572872 | tf_op jit(solution)/shard_map/ppermute | solution.py:143
